TPU v7x, 512 devices: a whole 4x8x8 slice. The times are simulated.
512 devices in a mesh: row: 32 (over z, x), col: 16 (over y, core).
Axes of the slice: x: 4, y: 8, z: 8, core: 2. Of those that a mesh axis runs over, the one named last changes fastest.
Arguments:
- src_points: bfloat16 [512, 64, 1024], P('row', 'col'), may hold values from -1.5 to 1.5
- dst_points: bfloat16 [64, 64, 1024], P('col', 'row'), may hold values from -1.5 to 1.5
- support: int32 [512, 8], P('row'), may hold values from 0 to 63, as said below
- log_src_mass: float32 [512, 1024], P('row'), may hold values from -1 to 1
- log_dst_mass: float32 [64, 1024], P('col'), may hold values from -1 to 1
- dst_potential: float32 [64, 1024], P('col'), may hold values from -4 to 114
Outputs:
- src_potential_new: float32 [512, 1024], P('row')
- dst_potential_new: float32 [64, 1024], P('col')
Inputs may be any that keep to these rules, and one draw needn't show every extreme that they name: `support`: each row cluster names 8 different column clusters; column cluster b belongs to col index b // 4; the col indices that one row cluster names lie in 3 cyclically consecutive indices of col, each of them named at least once; every column cluster is named by some row cluster; for every index of row and every index of col, at most 3 of the 16 row clusters of that row index name a column cluster of that col index, and some pair reaches 3.
All inputs are finite; a program needn't handle non-finite values.
Results may differ from a plain program's by a relative error of at most 0.0003.
Values may be sent and summed in bfloat16 or wider, within the bound.
No kernel may reach another device: no remote copies, remote signals or barrier semaphores. Data moves between devices by JAX's collectives and lax.ppermute only.
A program may use at most 64 MiB of HBM per device.

v0:
```python
import jax
import jax.numpy as jnp
from jax import lax
from jax.sharding import PartitionSpec as P

blur_scale = 0.5
floor_value = -1e30


def combine_parts(first_part, second_part):
    highest = jnp.maximum(first_part[0], second_part[0])
    totals = first_part[1] * jnp.exp(first_part[0] - highest) + second_part[1] * jnp.exp(
        second_part[0] - highest
    )
    return (highest, totals)


def tile_cost(src_full, dst_full, src_sq, dst_sq, row_id, col_id):
    left_side = lax.dynamic_index_in_dim(src_full, row_id, 0, keepdims=False)
    right_side = lax.dynamic_index_in_dim(dst_full, col_id, 0, keepdims=False)
    inner_prod = lax.dot_general(
        left_side, right_side, (((0,), (0,)), ((), ())), preferred_element_type=jnp.float32
    )
    left_sq = lax.dynamic_index_in_dim(src_sq, row_id, 0, keepdims=False)
    right_sq = lax.dynamic_index_in_dim(dst_sq, col_id, 0, keepdims=False)
    return left_sq[:, None] + right_sq[None, :] - 2.0 * inner_prod


def body(src_points, dst_points, support, log_src_mass, log_dst_mass, dst_potential):
    col_count = dst_points.shape[0]
    row_count = support.shape[0]
    per_row = support.shape[1]
    src_full = lax.all_gather(src_points, "col", axis=1, tiled=True)
    row_slot = jnp.arange(row_count, dtype=jnp.int32)
    dst_full = lax.all_gather(dst_points, "row", axis=1, tiled=True)
    src_vals = src_full.astype(jnp.float32)
    dst_vals = dst_full.astype(jnp.float32)
    src_sq = jnp.sum(src_vals * src_vals, axis=1)
    dst_sq = jnp.sum(dst_vals * dst_vals, axis=1)
    col_offset = lax.axis_index("col") * col_count
    chosen = support.reshape(-1)
    is_local = chosen // col_count == lax.axis_index("col")
    local_count = jnp.sum(is_local.astype(jnp.int32))
    sort_keys = jnp.where(is_local, 0, 1).astype(jnp.int32)
    entries = jnp.argsort(sort_keys, stable=True)

    def row_turn(turn_index, running):
        row_high, row_sum = running
        entry_id = entries[turn_index]
        row_id = entry_id // per_row
        col_id = chosen[entry_id] - col_offset
        costs = tile_cost(src_full, dst_full, src_sq, dst_sq, row_slot[row_id], col_id)
        potential = lax.dynamic_index_in_dim(dst_potential, col_id, 0, keepdims=False)
        scores = (potential[None, :] - costs) / blur_scale
        tile_high = jnp.max(scores, axis=1)
        tile_sum = jnp.sum(jnp.exp(scores - tile_high[:, None]), axis=1)
        old_high = lax.dynamic_index_in_dim(row_high, row_id, 0, keepdims=False)
        old_sum = lax.dynamic_index_in_dim(row_sum, row_id, 0, keepdims=False)
        new_high, new_sum = combine_parts((old_high, old_sum), (tile_high, tile_sum))
        row_high = lax.dynamic_update_index_in_dim(row_high, new_high, row_id, 0)
        row_sum = lax.dynamic_update_index_in_dim(row_sum, new_sum, row_id, 0)
        return (row_high, row_sum)

    row_start = (
        jnp.full(log_src_mass.shape, floor_value, jnp.float32),
        jnp.zeros(log_src_mass.shape, jnp.float32),
    )
    row_high, row_sum = lax.fori_loop(0, local_count, row_turn, row_start)
    whole_high = lax.pmax(row_high, "col")
    whole_sum = lax.psum(row_sum * jnp.exp(row_high - whole_high), "col")
    src_new = blur_scale * (log_src_mass - (whole_high + jnp.log(whole_sum)))

    def col_turn(turn_index, running):
        col_high, col_sum = running
        entry_id = entries[turn_index]
        row_id = entry_id // per_row
        col_id = chosen[entry_id] - col_offset
        costs = tile_cost(src_full, dst_full, src_sq, dst_sq, row_slot[row_id], col_id)
        potential = lax.dynamic_index_in_dim(src_new, row_id, 0, keepdims=False)
        scores = (potential[:, None] - costs) / blur_scale
        tile_high = jnp.max(scores, axis=0)
        tile_sum = jnp.sum(jnp.exp(scores - tile_high[None, :]), axis=0)
        old_high = lax.dynamic_index_in_dim(col_high, col_id, 0, keepdims=False)
        old_sum = lax.dynamic_index_in_dim(col_sum, col_id, 0, keepdims=False)
        new_high, new_sum = combine_parts((old_high, old_sum), (tile_high, tile_sum))
        col_high = lax.dynamic_update_index_in_dim(col_high, new_high, col_id, 0)
        col_sum = lax.dynamic_update_index_in_dim(col_sum, new_sum, col_id, 0)
        return (col_high, col_sum)

    col_start = (
        jnp.full(log_dst_mass.shape, floor_value, jnp.float32),
        jnp.zeros(log_dst_mass.shape, jnp.float32),
    )
    col_high, col_sum = lax.fori_loop(0, local_count, col_turn, col_start)
    final_high = lax.pmax(col_high, "row")
    final_sum = lax.psum(col_sum * jnp.exp(col_high - final_high), "row")
    dst_new = blur_scale * (log_dst_mass - (final_high + jnp.log(final_sum)))
    return (src_new, dst_new)


def solution(mesh):
    return jax.shard_map(
        body,
        mesh=mesh,
        in_specs=(
            P("row", "col", None),
            P("col", "row", None),
            P("row", None),
            P("row", None),
            P("col", None),
            P("col", None),
        ),
        out_specs=(P("row", None), P("col", None)),
        check_vma=False,
    )
```

profile of v0, /device:TPU:6, one launch (start us, length us, event | category | flops | bytes accessed | tf_op | source)
XLA Modules:
  0.0 864.4 jit_solution(8652787842201760324)
XLA Ops:
  7.2 1.6 copy.11
  10.5 55.3 %all_gather.7 = bf16[4,64,1024]{2,0,1:T(4,128)(2,1)S(1)} all-gather(bf16[4,2,1024]{2,0,1:T(4,128)(2,1)S(1)} %copy.12), channel_id=1, replica_groups=mesh['row'=32,'col'=16] {'row'}, dimensions={1}, use_global_device_ids=true | all-gather | bytes 540672 | tf_op jit(solution)/shard_map/all_gather | solution.py:35
  65.9 2.5 sort.17
  68.5 1.4 convert_reduce_fusion
  70.2 2.9 copy.13
  73.6 145.2 %while.28 = (s32[]{:T(128)}, f32[16,1024]{1,0:T(8,128)S(1)}, f32[16,1024]{1,0:T(8,128)S(1)}, s32[]{:T(128)}, s32[128]{0:T(128)S(1)}, /*index=5*/s32[128]{0:T(128...) while((s32[]{:T(128)}, f32[16,1024]{1,0:T(8,128)S(1)}, ...), condition=%wide.region_7.8_spmd, body=%wide.region_4.7_spmd.sunk | while | flops 147853344 | bytes 8753732 | solution.py:68
  83.6 1.1 fusion.19
  84.7 1.8 exponential_reduce_fusion.4
  96.7 1.1 fusion.19
  97.9 1.8 exponential_reduce_fusion.4
  109.8 1.1 fusion.19
  111.0 1.8 exponential_reduce_fusion.4
  123.0 1.1 fusion.19
  124.1 1.8 exponential_reduce_fusion.4
  136.1 1.1 fusion.19
  137.3 1.8 exponential_reduce_fusion.4
  149.2 1.1 fusion.19
  150.4 1.8 exponential_reduce_fusion.4
  162.4 1.1 fusion.19
  163.5 1.8 exponential_reduce_fusion.4
  175.5 1.1 fusion.19
  176.7 1.8 exponential_reduce_fusion.4
  188.6 1.1 fusion.19
  189.8 1.8 exponential_reduce_fusion.4
  201.8 1.1 fusion.19
  202.9 1.8 exponential_reduce_fusion.4
  214.9 1.1 fusion.19
  216.1 1.8 exponential_reduce_fusion.4
  219.5 111.0 %all-reduce.3.cloned.1.call-done = f32[16,1024]{1,0:T(8,128)} async-done(((f32[16,1024]{1,0:T(8,128)}), f32[16,1024]{1,0:T(8,128)}) %all-reduce.3.cloned.1.call-update) | async-done | bytes 65552 | tf_op jit(solution)/shard_map/pmax | solution.py:69
  330.5 1.5 exponential_multiply_fusion
  332.1 106.6 %all-reduce.5.cloned.1.call-done = f32[16,1024]{1,0:T(8,128)} async-done(((f32[16,1024]{1,0:T(8,128)}), f32[16,1024]{1,0:T(8,128)}) %all-reduce.5.cloned.1.call-update) | async-done | bytes 65552 | tf_op jit(solution)/shard_map/psum | solution.py:70
  439.6 135.9 %while.29 = (s32[]{:T(128)}, f32[4,1024]{1,0:T(4,128)S(1)}, f32[4,1024]{1,0:T(4,128)S(1)}, s32[]{:T(128)}, s32[128]{0:T(128)S(1)}, /*index=5*/s32[128]{0:T(128)S...) while((s32[]{:T(128)}, f32[4,1024]{1,0:T(4,128)S(1)}, ...), condition=%wide.region_13.14_spmd, body=%wide.region_10.13_spmd.sunk | while | flops 147853344 | bytes 8753732 | solution.py:94
  449.9 1.8 exponential_reduce_fusion.5
  462.2 1.8 exponential_reduce_fusion.5
  473.4 1.1 fusion.20
  474.5 1.8 exponential_reduce_fusion.5
  485.7 1.1 fusion.20
  486.8 1.8 exponential_reduce_fusion.5
  498.0 1.1 fusion.20
  499.1 1.8 exponential_reduce_fusion.5
  511.4 1.8 exponential_reduce_fusion.5
  523.7 1.8 exponential_reduce_fusion.5
  536.0 1.8 exponential_reduce_fusion.5
  548.2 1.8 exponential_reduce_fusion.5
  560.5 1.8 exponential_reduce_fusion.5
  572.8 1.8 exponential_reduce_fusion.5
  575.5 141.8 %pmax.15 = f32[4,1024]{1,0:T(4,128)S(1)} all-reduce(f32[4,1024]{1,0:T(4,128)S(1)} %get-tuple-element.338), channel_id=1, replica_groups=mesh['row'=32,'col'=16] {'row'}, use_global_device_ids=true, to_apply=%region_14.15 | all-reduce | flops 4096 | bytes 32768 | tf_op jit(solution)/shard_map/pmax | solution.py:95
  717.3 139.9 %psum.15 = f32[4,1024]{1,0:T(4,128)S(1)} all-reduce(f32[4,1024]{1,0:T(4,128)S(1)} %exponential_multiply_fusion.1), channel_id=1, replica_groups=mesh['row'=32,'col'=16] {'row'}, use_global_device_ids=true, to_apply=%region_15.16 | all-reduce | flops 4096 | bytes 32768 | tf_op jit(solution)/shard_map/psum | solution.py:96
  (218 shorter events, 67.2 us)
Async XLA Ops:
  7.2 63.0 %all-gather.2.cloned.1.call-start = ((), (), s32[]{:S(2)}) async-start(), calls=%async_computation | async-start | bytes 2228224 | tf_op jit(solution)/shard_map/all_gather | solution.py:33
  8.8 321.7 %all-reduce.3.cloned.1.call-start = ((), (), s32[]{:S(2)}) async-start(), calls=%async_computation.1 | async-start | bytes 131072 | tf_op jit(solution)/shard_map/pmax | solution.py:69
  70.2 2.9 copy-start
  73.6 365.1 %copy-start.3 = (f32[16,1024]{1,0:T(8,128)S(1)}, f32[16,1024]{1,0:T(8,128)}, u32[]{:S(2)}) copy-start(f32[16,1024]{1,0:T(8,128)} %param.13) | copy-start | bytes 196612
  218.8 0.6 copy-start.1
  219.5 219.2 %all-reduce.5.cloned.1.call-start = ((), (), s32[]{:S(2)}) async-start(), calls=%async_computation.2 | async-start | bytes 131072 | tf_op jit(solution)/shard_map/psum | solution.py:70
  439.6 417.6 %copy-start.4 = (f32[4,1024]{1,0:T(4,128)S(1)}, f32[4,1024]{1,0:T(4,128)}, u32[]{:S(2)}) copy-start(f32[4,1024]{1,0:T(4,128)} %param.14) | copy-start | bytes 49156
  575.5 282.3 %copy-start.2 = (f32[16,1024]{1,0:T(8,128)}, f32[16,1024]{1,0:T(8,128)S(1)}, u32[]{:S(2)}) copy-start(f32[16,1024]{1,0:T(8,128)S(1)} %get-tuple-element.755) | copy-start | bytes 196612
Sparse Core Ops, SparseCore 0:
  10.1 46.3 all-gather.1
  219.6 110.8 all-reduce.2
  333.4 105.1 all-reduce.4
where the time goes:
time: 872 us; the launch traced here: 864 us
  blocking collectives  337 us (39%)
  waiting for transfers between devices  218 us (25%)
  loops' own time  164 us (19%)
  local copies, waits for them, and re-layouts  59.9 us (7%)
  other arithmetic  47.7 us (5%)
  matrix products  24.3 us (3%)
  between operations  13.9 us (2%)
    pmax x1, blocking collectives, body(): final_high = lax.pmax(col_high, 'row')  142 us
    psum x1, blocking collectives, body(): final_sum = lax.psum(col_sum * jnp.exp(col_high - final_high), 'row')  140 us
    pmax x1, waiting for transfers between devices, body(): whole_high = lax.pmax(row_high, 'col')  111 us
    psum x1, waiting for transfers between devices, body(): whole_sum = lax.psum(row_sum * jnp.exp(row_high - whole_high), 'col')  107 us
    another operation x1, loops' own time, body(): col_high, col_sum = lax.fori_loop(0, local_count, col_turn, col_start)  81.9 us
    another operation x1, loops' own time, body(): row_high, row_sum = lax.fori_loop(0, local_count, row_turn, row_start)  81.9 us
    all_gather x1, blocking collectives, body(): dst_full = lax.all_gather(dst_points, 'row', axis=1, tiled=True)  55.3 us
    dot_general x22, matrix products, tile_cost(): lax.dot_general(left_side, right_side, (((0,), (0,)), ((), ())), preferre...  24.3 us
  transfers between devices with their start and end apart: 3, of which 2 were waited for; matrix products, arithmetic and copies ran while one was open for 1% of the time, Pallas kernels for 0%

commit v1 on v0

v1 whole, which is shorter than its diff:
```python
import functools

import jax
import jax.numpy as jnp
from jax import lax
from jax.experimental import pallas as pl
from jax.experimental.pallas import tpu as pltpu
from jax.sharding import PartitionSpec as P

blur_scale = 0.5
floor_value = -1e30
SLOTS = 3
CHUNK = 256


def tile_kernel(lhs_ref, bias_ref, rhs_ref, out_ref):
    reduced = lhs_ref.shape[1]
    kept = rhs_ref.shape[2]
    rhs = rhs_ref[0]

    def chunk(ci, carry):
        high, total = carry
        start = pl.multiple_of(ci * CHUNK, CHUNK)
        left = lhs_ref[0, pl.ds(start, CHUNK), :]
        vals = jnp.dot(left, rhs, preferred_element_type=jnp.float32)
        vals = vals + bias_ref[0, pl.ds(start, CHUNK), :]
        new_high = jnp.maximum(high, jnp.max(vals, axis=0, keepdims=True))
        total = total * jnp.exp(high - new_high) + jnp.sum(
            jnp.exp(vals - new_high), axis=0, keepdims=True
        )
        return new_high, total

    start = (
        jnp.full((1, kept), floor_value, jnp.float32),
        jnp.zeros((1, kept), jnp.float32),
    )
    high, total = lax.fori_loop(0, reduced // CHUNK, chunk, start, unroll=True)
    out_ref[0, 0] = high + jnp.log(total)


def tile_lse(lhs, bias, rhs, lhs_by_slot):
    n_lhs, reduced, depth = lhs.shape
    n_rhs, _, kept = rhs.shape
    slots, n_cc = (n_lhs, n_rhs) if lhs_by_slot else (n_rhs, n_lhs)
    if lhs_by_slot:
        lhs_map = lambda s, k: (s, 0, 0)
        rhs_map = lambda s, k: (k, 0, 0)
    else:
        lhs_map = lambda s, k: (k, 0, 0)
        rhs_map = lambda s, k: (s, 0, 0)
    return pl.pallas_call(
        tile_kernel,
        grid=(slots, n_cc),
        in_specs=[
            pl.BlockSpec((1, reduced, depth), lhs_map),
            pl.BlockSpec((1, reduced, 1), lhs_map),
            pl.BlockSpec((1, depth, kept), rhs_map),
        ],
        out_specs=pl.BlockSpec((1, 1, 1, kept), lambda s, k: (s, k, 0, 0)),
        out_shape=jax.ShapeDtypeStruct((slots, n_cc, 1, kept), jnp.float32),
    )(lhs, bias, rhs)


def masked_lse(values, mask, axis):
    high = jnp.max(jnp.where(mask, values, floor_value), axis=axis)
    total = jnp.sum(
        jnp.where(mask, jnp.exp(values - jnp.expand_dims(high, axis)), 0.0), axis=axis
    )
    return jnp.where(jnp.any(mask, axis=axis), high + jnp.log(total), floor_value)


def log_add(first, second):
    high = jnp.maximum(first, second)
    return high + jnp.log(jnp.exp(first - high) + jnp.exp(second - high))


def body(src_points, dst_points, support, log_src_mass, log_dst_mass, dst_potential, n_row, n_col):
    row_count, dim_part, pts = src_points.shape
    col_count = dst_points.shape[0]
    col_id = lax.axis_index("col")

    dst_full = lax.all_gather(dst_points, "row", axis=1, tiled=True)

    dev_of = support // col_count
    touches = jnp.any(
        dev_of[:, :, None] == jnp.arange(n_col, dtype=jnp.int32)[None, None, :], axis=1
    )
    rank = jnp.cumsum(touches.astype(jnp.int32), axis=0) - 1
    onehot = touches.T[:, None, :] & (
        rank.T[:, None, :] == jnp.arange(SLOTS, dtype=jnp.int32)[None, :, None]
    )
    table = jnp.sum(
        onehot.astype(jnp.int32) * jnp.arange(row_count, dtype=jnp.int32)[None, None, :], axis=2
    )
    slot_ok = jnp.any(onehot, axis=2)

    send = jnp.take(src_points, table.reshape(-1), axis=0).reshape(
        n_col, SLOTS, dim_part, pts
    )
    recv = lax.all_to_all(send, "col", 0, 0, tiled=True)
    src_mine = recv.transpose(1, 0, 2, 3).reshape(SLOTS, n_col * dim_part, pts)

    my_table = lax.dynamic_index_in_dim(table, col_id, 0, keepdims=False)
    my_ok = lax.dynamic_index_in_dim(slot_ok, col_id, 0, keepdims=False)
    my_support = jnp.take(support, my_table, axis=0)
    valid = my_ok[:, None] & jnp.any(
        my_support[:, None, :]
        == (col_id * col_count + jnp.arange(col_count, dtype=jnp.int32))[None, :, None],
        axis=2,
    )

    src_vals = src_mine.astype(jnp.float32)
    src_sq = jnp.sum(src_vals * src_vals, axis=1)
    dst_vals = dst_full.astype(jnp.float32)
    dst_sq = jnp.sum(dst_vals * dst_vals, axis=1)

    dst_lhs = (dst_full * 4).transpose(0, 2, 1)
    dst_bias = (2.0 * dst_potential - 2.0 * dst_sq)[:, :, None]
    row_tiles = tile_lse(dst_lhs, dst_bias, src_mine, lhs_by_slot=False)[:, :, 0, :]
    row_local = masked_lse(row_tiles, valid[:, :, None], axis=1) - 2.0 * src_sq
    row_local = jnp.where(my_ok[:, None], row_local, floor_value)

    row_all = lax.all_gather(row_local, "col", axis=0, tiled=False)
    owner = onehot.transpose(2, 0, 1)
    whole = masked_lse(
        jnp.broadcast_to(row_all[None], (row_count, n_col, SLOTS, pts)).reshape(row_count, n_col * SLOTS, pts),
        owner.reshape(row_count, n_col * SLOTS)[:, :, None],
        axis=1,
    )
    src_new = blur_scale * (log_src_mass - whole)

    my_pot = jnp.take(src_new, my_table, axis=0)
    src_lhs = (src_mine * 4).transpose(0, 2, 1)
    src_bias = (2.0 * my_pot - 2.0 * src_sq)[:, :, None]
    col_tiles = tile_lse(src_lhs, src_bias, dst_full, lhs_by_slot=True)[:, :, 0, :]
    col_local = masked_lse(col_tiles, valid[:, :, None], axis=0)

    step = 1
    while step < n_row:
        partner = lax.ppermute(col_local, "row", [(i, i ^ step) for i in range(n_row)])
        col_local = log_add(col_local, partner)
        step *= 2
    dst_new = blur_scale * (log_dst_mass - (col_local - 2.0 * dst_sq))
    return (src_new, dst_new)


def solution(mesh):
    n_row = mesh.shape["row"]
    n_col = mesh.shape["col"]
    return jax.shard_map(
        functools.partial(body, n_row=n_row, n_col=n_col),
        mesh=mesh,
        in_specs=(
            P("row", "col", None),
            P("col", "row", None),
            P("row", None),
            P("row", None),
            P("col", None),
            P("col", None),
        ),
        out_specs=(P("row", None), P("col", None)),
        check_vma=False,
    )
```

time: 872 us -> 175 us (0.20)
  blocking collectives: 337 us -> 73.2 us
  waiting for transfers between devices: 218 us -> 21 us
  loops' own time: 164 us -> 0 us
  local copies, waits for them, and re-layouts: 59.9 us -> 9.23 us
  Pallas kernels: 0 us -> 35.1 us
  other arithmetic: 47.7 us -> 14.1 us
  matrix products: 24.3 us -> 0 us
  starting transfers between devices: 0.12 us -> 20.6 us
  between operations: 13.9 us -> 0.91 us
    another operation x2 -> x0, loops' own time: 164 us -> none  [the longest x1 81.9 us: body(): col_high, col_sum = lax.fori_loop(0, local_count, col_turn, col_start)]
    pmax x1 -> x0, blocking collectives: 142 us -> none  [body(): final_high = lax.pmax(col_high, 'row')]
    psum x1 -> x0, blocking collectives: 140 us -> none  [body(): final_sum = lax.psum(col_sum * jnp.exp(col_high - final_high), 'row')]
    pmax x1 -> x0, waiting for transfers between devices: 111 us -> none  [body(): whole_high = lax.pmax(row_high, 'col')]
    psum x1 -> x0, waiting for transfers between devices: 107 us -> none  [body(): whole_sum = lax.psum(row_sum * jnp.exp(row_high - whole_high), 'col')]
    dynamic_slice x110 -> x2, local copies, waits for them, and re-layouts: 49 us -> 0.37 us  [the longest x1 0.19 us: body(): my_ok = lax.dynamic_index_in_dim(slot_ok, col_id, 0, keepdims=False)]
    reduce_sum x23 -> x4, other arithmetic: 40.6 us -> 2.77 us  [the longest x3 2.61 us: masked_lse(): jnp.sum(jnp.where(mask, jnp.exp(values - jnp.expand_dims(high, axis)), 0....]
    pallas_call x0 -> x2, Pallas kernels: none -> 35.1 us  [tile_lse(): pl.pallas_call(tile_kernel, grid=(slots, n_cc), in_specs=[pl.BlockSpec((1...]
  transfers between devices with their start and end apart: 3 -> 6, of which waited for: 2 -> 5; matrix products, arithmetic and copies ran while one was open for 1% -> 4% of each run, Pallas kernels for 0% -> 0%
where the time goes in v1:
time: 175 us; the launch traced here: 174 us
  blocking collectives  73.2 us (42%)
  Pallas kernels  35.1 us (20%)
  waiting for transfers between devices  21 us (12%)
  starting transfers between devices  20.6 us (12%)
  other arithmetic  14.1 us (8%)
  local copies, waits for them, and re-layouts  9.23 us (5%)
    all_gather x1, blocking collectives, body(): dst_full = lax.all_gather(dst_points, 'row', axis=1, tiled=True)  55.2 us
    pallas_call x2, Pallas kernels, tile_lse(): pl.pallas_call(tile_kernel, grid=(slots, n_cc), in_specs=[pl.BlockSpec((1...  35.1 us
    ppermute x5, waiting for transfers between devices, body(): lax.ppermute(col_local, 'row', [(i, i ^ step) for i in range(n_row)])  21 us
    all_gather x1, blocking collectives, body(): row_all = lax.all_gather(row_local, 'col', axis=0, tiled=False)  18 us
    ppermute x5, starting transfers between devices, body(): lax.ppermute(col_local, 'row', [(i, i ^ step) for i in range(n_row)])  13.4 us
    all_to_all x1, starting transfers between devices, body(): recv = lax.all_to_all(send, 'col', 0, 0, tiled=True)  7.21 us
  transfers between devices with their start and end apart: 6, of which 5 were waited for; matrix products, arithmetic and copies ran while one was open for 4% of the time, Pallas kernels for 0%

profile of v1, /device:TPU:6, one launch (start us, length us, event | category | flops | bytes accessed | tf_op | source)
XLA Modules:
  0.0 174.2 jit_solution(10525327969651099198)
XLA Ops:
  0.7 0.8 add_select_fusion.1
  1.5 0.1 fusion
  1.8 0.2 select_reduce_fusion.2
  2.3 0.9 gather_fusion.1
  3.2 1.0 broadcast_select_fusion
  4.2 7.2 %all-to-all-start = ((bf16[16,3,4,1024]{3,2,1,0:T(4,128)(2,1)}), bf16[16,3,4,1024]{3,2,1,0:T(4,128)(2,1)S(1)}, u32[]{:S(2)}, u32[]{:S(2)}) async-start(bf16[16,3,4,1024]{3,2,1,0:T(4,128)(2,1)} %broadcast_select_fusion), calls=%async_computation | async-start | bytes 786432 | tf_op jit(solution)/shard_map/all_to_all | solution.py:100
  11.5 0.2 dynamic-slice_reduce_fusion
  11.7 55.2 %all_gather.7 = bf16[4,64,1024]{2,0,1:T(4,128)(2,1)S(1)} all-gather(bf16[4,2,1024]{2,0,1:T(4,128)(2,1)S(1)} %copy.76), channel_id=1, replica_groups=mesh['row'=32,'col'=16] {'row'}, dimensions={1}, use_global_device_ids=true | all-gather | bytes 540672 | tf_op jit(solution)/shard_map/all_gather | solution.py:82
  67.0 0.3 multiply_reduce_fusion
  67.3 0.1 fusion.24
  67.4 0.6 gather_fusion
  68.1 0.1 fusion.11
  68.2 0.7 copy.77
  69.0 1.0 copy.89.rhs_ref
  69.9 0.2 dynamic-slice_reduce_fusion.1
  70.1 2.0 %copy.82.bias_ref = f32[4,1024,1]{2,1,0:T(8,128)} copy(f32[4,1024,1]{1,0,2:T(4,128)S(1)} %subtract_bitcast_fusion) | data formatting | bytes 32768 | tf_op jit(solution)/shard_map/broadcast_in_dim | solution.py:118
  72.1 0.2 compare_reduce_fusion
  72.3 0.2 fusion.23
  72.5 1.1 multiply_bitcast_fusion.lhs_ref
  73.6 0.1 copy.81
  73.9 1.2 copy.84
  75.0 17.5 %shard_map.77 = f32[3,4,1,1024]{3,2,1,0:T(1,128)} custom-call(bf16[4,1024,64]{2,1,0:T(8,128)(2,1)} %multiply_bitcast_fusion.lhs_ref, f32[4,1024,1]{2,1,0:T(8,128)} %copy.82.bias_ref, bf16[3,64,1024]{2,1,0:T(8,128)(2,1)} %copy-done.1), custom_call_target="tpu_custom_call" | custom-call | tf_op jit(solution)/shard_map/pallas_call | solution.py:51
  92.6 0.9 fusion.5
  93.5 0.9 fusion.8
  94.4 0.2 multiply_reduce_fusion.1
  94.8 18.0 %all_gather.8 = f32[16,3,1024]{2,1,0:T(4,128)S(1)} all-gather(f32[1,3,1024]{2,1,0:T(4,128)S(1)} %fusion.12), channel_id=1, replica_groups=mesh['row'=32,'col'=16] {'col'}, dimensions={0}, use_global_device_ids=true | all-gather | bytes 208896 | tf_op jit(solution)/shard_map/all_gather | solution.py:123
  112.7 0.1 copy.83
  112.9 0.7 select_reduce_fusion.1
  113.5 0.8 select_reduce_fusion
  114.5 0.6 gather_fusion.2
  115.0 0.5 copy.86
  115.5 0.5 copy.88
  116.0 2.1 %multiply_bitcast_fusion.1.lhs_ref = bf16[3,1024,64]{2,1,0:T(8,128)(2,1)} fusion(bf16[3,64,1024]{1,2,0:T(8,128)(2,1)} %copy.84), kind=kLoop, calls=%fused_computation.8 | loop fusion | flops 196608 | bytes 786432 | tf_op jit(solution)/shard_map/transpose | solution.py:133
  118.1 1.4 multiply_subtract_fusion.bias_ref
  119.5 17.5 %shard_map.78 = f32[3,4,1,1024]{3,2,1,0:T(1,128)} custom-call(bf16[3,1024,64]{2,1,0:T(8,128)(2,1)} %multiply_bitcast_fusion.1.lhs_ref, f32[3,1024,1]{2,1,0:T(8,128)} %multiply_subtract_fusion.bias_ref, bf16[4,64,1024]{2,1,0:T(8,128)(2,1)} %copy.89.rhs_ref), custom_call_target="tpu_custom_call" | custom-call | tf_op jit(solution)/shard_map/pallas_call | solution.py:51
  137.1 0.9 fusion.1
  138.0 0.9 fusion.4
  138.9 2.7 %collective-permute-start = (f32[4,1024]{1,0:T(4,128)S(1)}, f32[4,1024]{1,0:T(4,128)S(1)}, u32[]{:S(2)}, u32[]{:S(2)}) collective-permute-start(f32[4,1024]{1,0:T(4,128)S(1)} %add_select_fusion), channel_id=1, source_target_pairs={{0,16},{16,0},{32,48},{48,32},{64,80},{80,64},{96,112},{112,96},{1... | collective-permute-start | bytes 49160 | tf_op jit(solution)/shard_map/ppermute | solution.py:140
  141.6 2.9 %collective-permute-done = f32[4,1024]{1,0:T(4,128)S(1)} collective-permute-done((f32[4,1024]{1,0:T(4,128)S(1)}, f32[4,1024]{1,0:T(4,128)S(1)}, u32[]{:S(2)}, u32[]{:S(2)}) %collective-permute-start) | collective-permute-done | bytes 16416 | tf_op jit(solution)/shard_map/ppermute | solution.py:140
  144.6 3.4 %collective-permute-start.1 = (f32[4,1024]{1,0:T(4,128)S(1)}, f32[4,1024]{1,0:T(4,128)S(1)}, u32[]{:S(2)}, u32[]{:S(2)}) collective-permute-start(f32[4,1024]{1,0:T(4,128)S(1)} %log_add_fusion.3), channel_id=1, source_target_pairs={{0,32},{16,48},{32,0},{48,16},{64,96},{80,112},{96,64},{112,80},{1... | collective-permute-start | bytes 49160 | tf_op jit(solution)/shard_map/ppermute | solution.py:140
  148.0 3.7 %collective-permute-done.1 = f32[4,1024]{1,0:T(4,128)S(1)} collective-permute-done((f32[4,1024]{1,0:T(4,128)S(1)}, f32[4,1024]{1,0:T(4,128)S(1)}, u32[]{:S(2)}, u32[]{:S(2)}) %collective-permute-start.1) | collective-permute-done | bytes 16416 | tf_op jit(solution)/shard_map/ppermute | solution.py:140
  151.7 1.9 %collective-permute-start.2 = (f32[4,1024]{1,0:T(4,128)S(1)}, f32[4,1024]{1,0:T(4,128)S(1)}, u32[]{:S(2)}, u32[]{:S(2)}) collective-permute-start(f32[4,1024]{1,0:T(4,128)S(1)} %log_add_fusion.2), channel_id=1, source_target_pairs={{0,64},{16,80},{32,96},{48,112},{64,0},{80,16},{96,32},{112,48},{1... | collective-permute-start | bytes 49160 | tf_op jit(solution)/shard_map/ppermute | solution.py:140
  153.7 3.7 %collective-permute-done.2 = f32[4,1024]{1,0:T(4,128)S(1)} collective-permute-done((f32[4,1024]{1,0:T(4,128)S(1)}, f32[4,1024]{1,0:T(4,128)S(1)}, u32[]{:S(2)}, u32[]{:S(2)}) %collective-permute-start.2) | collective-permute-done | bytes 16416 | tf_op jit(solution)/shard_map/ppermute | solution.py:140
  157.4 2.1 %collective-permute-start.3 = (f32[4,1024]{1,0:T(4,128)S(1)}, f32[4,1024]{1,0:T(4,128)S(1)}, u32[]{:S(2)}, u32[]{:S(2)}) collective-permute-start(f32[4,1024]{1,0:T(4,128)S(1)} %log_add_fusion.1), channel_id=1, source_target_pairs={{0,128},{16,144},{32,160},{48,176},{64,192},{80,208},{96,224},{112... | collective-permute-start | bytes 49160 | tf_op jit(solution)/shard_map/ppermute | solution.py:140
  159.5 4.4 %collective-permute-done.3 = f32[4,1024]{1,0:T(4,128)S(1)} collective-permute-done((f32[4,1024]{1,0:T(4,128)S(1)}, f32[4,1024]{1,0:T(4,128)S(1)}, u32[]{:S(2)}, u32[]{:S(2)}) %collective-permute-start.3) | collective-permute-done | bytes 16416 | tf_op jit(solution)/shard_map/ppermute | solution.py:140
  164.0 3.3 %collective-permute-start.4 = (f32[4,1024]{1,0:T(4,128)S(1)}, f32[4,1024]{1,0:T(4,128)S(1)}, u32[]{:S(2)}, u32[]{:S(2)}) collective-permute-start(f32[4,1024]{1,0:T(4,128)S(1)} %log_add_fusion), channel_id=1, source_target_pairs={{0,256},{16,272},{32,288},{48,304},{64,320},{80,336},{96,352},{112... | collective-permute-start | bytes 49160 | tf_op jit(solution)/shard_map/ppermute | solution.py:140
  167.3 6.2 %collective-permute-done.4 = f32[4,1024]{1,0:T(4,128)S(1)} collective-permute-done((f32[4,1024]{1,0:T(4,128)S(1)}, f32[4,1024]{1,0:T(4,128)S(1)}, u32[]{:S(2)}, u32[]{:S(2)}) %collective-permute-start.4) | collective-permute-done | bytes 16416 | tf_op jit(solution)/shard_map/ppermute | solution.py:140
  173.5 0.6 subtract_multiply_fusion.1
  (47 shorter events, 1.3 us)
Async XLA Ops:
  0.6 1.7 copy-start
  0.6 10.8 %copy-start.6 = (s32[16,8]{0,1:T(8,128)S(1)}, s32[16,8]{0,1:T(8,128)}, u32[]{:S(2)}) copy-start(s32[16,8]{0,1:T(8,128)} %param.8) | copy-start | bytes 1540
  0.7 11.1 %copy-start.7 = (bf16[4,2,1024]{2,1,0:T(2,128)(2,1)S(1)}, bf16[4,2,1024]{2,1,0:T(2,128)(2,1)}, u32[]{:S(2)}) copy-start(bf16[4,2,1024]{2,1,0:T(2,128)(2,1)} %param.7) | copy-start | bytes 49156
  0.7 67.4 %copy-start.4 = (f32[4,1024]{1,0:T(4,128)S(1)}, f32[4,1024]{1,0:T(4,128)}, u32[]{:S(2)}) copy-start(f32[4,1024]{1,0:T(4,128)} %param.11) | copy-start | bytes 49156
  4.2 69.4 %all-to-all-start = ((bf16[16,3,4,1024]{3,2,1,0:T(4,128)(2,1)}), bf16[16,3,4,1024]{3,2,1,0:T(4,128)(2,1)S(1)}, u32[]{:S(2)}, u32[]{:S(2)}) async-start(bf16[16,3,4,1024]{3,2,1,0:T(4,128)(2,1)} %broadcast_select_fusion), calls=%async_computation | async-start | bytes 786432 | tf_op jit(solution)/shard_map/all_to_all | solution.py:100
  73.9 1.2 copy-start.1
  92.6 21.8 %copy-start.3 = (f32[16,1024]{1,0:T(8,128)S(1)}, f32[16,1024]{1,0:T(8,128)}, u32[]{:S(2)}) copy-start(f32[16,1024]{1,0:T(8,128)} %param.9) | copy-start | bytes 196612
  114.4 3.7 %copy-start.2 = (f32[16,1024]{1,0:T(8,128)}, f32[16,1024]{1,0:T(8,128)S(1)}, u32[]{:S(2)}) copy-start(f32[16,1024]{1,0:T(8,128)S(1)} %subtract_multiply_fusion) | copy-start | bytes 196612
  119.5 54.0 %copy-start.5 = (f32[4,1024]{1,0:T(4,128)S(1)}, f32[4,1024]{1,0:T(4,128)}, u32[]{:S(2)}) copy-start(f32[4,1024]{1,0:T(4,128)} %param.10) | copy-start | bytes 49156
  138.9 5.6 %collective-permute-start = (f32[4,1024]{1,0:T(4,128)S(1)}, f32[4,1024]{1,0:T(4,128)S(1)}, u32[]{:S(2)}, u32[]{:S(2)}) collective-permute-start(f32[4,1024]{1,0:T(4,128)S(1)} %add_select_fusion), channel_id=1, source_target_pairs={{0,16},{16,0},{32,48},{48,32},{64,80},{80,64},{96,112},{112,96},{1... | collective-permute-start | bytes 49160 | tf_op jit(solution)/shard_map/ppermute | solution.py:140
  144.6 7.1 %collective-permute-start.1 = (f32[4,1024]{1,0:T(4,128)S(1)}, f32[4,1024]{1,0:T(4,128)S(1)}, u32[]{:S(2)}, u32[]{:S(2)}) collective-permute-start(f32[4,1024]{1,0:T(4,128)S(1)} %log_add_fusion.3), channel_id=1, source_target_pairs={{0,32},{16,48},{32,0},{48,16},{64,96},{80,112},{96,64},{112,80},{1... | collective-permute-start | bytes 49160 | tf_op jit(solution)/shard_map/ppermute | solution.py:140
  151.7 5.6 %collective-permute-start.2 = (f32[4,1024]{1,0:T(4,128)S(1)}, f32[4,1024]{1,0:T(4,128)S(1)}, u32[]{:S(2)}, u32[]{:S(2)}) collective-permute-start(f32[4,1024]{1,0:T(4,128)S(1)} %log_add_fusion.2), channel_id=1, source_target_pairs={{0,64},{16,80},{32,96},{48,112},{64,0},{80,16},{96,32},{112,48},{1... | collective-permute-start | bytes 49160 | tf_op jit(solution)/shard_map/ppermute | solution.py:140
  157.4 6.5 %collective-permute-start.3 = (f32[4,1024]{1,0:T(4,128)S(1)}, f32[4,1024]{1,0:T(4,128)S(1)}, u32[]{:S(2)}, u32[]{:S(2)}) collective-permute-start(f32[4,1024]{1,0:T(4,128)S(1)} %log_add_fusion.1), channel_id=1, source_target_pairs={{0,128},{16,144},{32,160},{48,176},{64,192},{80,208},{96,224},{112... | collective-permute-start | bytes 49160 | tf_op jit(solution)/shard_map/ppermute | solution.py:140
  164.0 9.5 %collective-permute-start.4 = (f32[4,1024]{1,0:T(4,128)S(1)}, f32[4,1024]{1,0:T(4,128)S(1)}, u32[]{:S(2)}, u32[]{:S(2)}) collective-permute-start(f32[4,1024]{1,0:T(4,128)S(1)} %log_add_fusion), channel_id=1, source_target_pairs={{0,256},{16,272},{32,288},{48,304},{64,320},{80,336},{96,352},{112... | collective-permute-start | bytes 49160 | tf_op jit(solution)/shard_map/ppermute | solution.py:140

commit v2 on v1

--- a/solution.py
+++ b/solution.py
@@ -79,7 +79,9 @@
     col_count = dst_points.shape[0]
     col_id = lax.axis_index("col")
 
-    dst_full = lax.all_gather(dst_points, "row", axis=1, tiled=True)
+    dst_copies = jnp.broadcast_to(dst_points[None], (n_row,) + dst_points.shape)
+    dst_recv = lax.all_to_all(dst_copies, "row", 0, 0, tiled=True)
+    dst_full = dst_recv.transpose(1, 0, 2, 3).reshape(col_count, -1, dst_points.shape[2])
 
     dev_of = support // col_count
     touches = jnp.any(
@@ -135,12 +137,11 @@
     col_tiles = tile_lse(src_lhs, src_bias, dst_full, lhs_by_slot=True)[:, :, 0, :]
     col_local = masked_lse(col_tiles, valid[:, :, None], axis=0)
 
-    step = 1
-    while step < n_row:
-        partner = lax.ppermute(col_local, "row", [(i, i ^ step) for i in range(n_row)])
-        col_local = log_add(col_local, partner)
-        step *= 2
-    dst_new = blur_scale * (log_dst_mass - (col_local - 2.0 * dst_sq))
+    col_copies = jnp.broadcast_to(col_local[None], (n_row,) + col_local.shape)
+    col_all = lax.all_to_all(col_copies, "row", 0, 0, tiled=True)
+    col_high = jnp.max(col_all, axis=0)
+    col_whole = col_high + jnp.log(jnp.sum(jnp.exp(col_all - col_high[None]), axis=0))
+    dst_new = blur_scale * (log_dst_mass - (col_whole - 2.0 * dst_sq))
     return (src_new, dst_new)
 
 

time: 175 us -> 146 us (0.83)
  blocking collectives: 73.2 us -> 37.7 us
  waiting for transfers between devices: 21 us -> 27.3 us
    all_gather x1 -> x0, blocking collectives: 55.2 us -> none  [body(): dst_full = lax.all_gather(dst_points, 'row', axis=1, tiled=True)]
    all_to_all x0 -> x1, blocking collectives: none -> 22.7 us  [body(): col_all = lax.all_to_all(col_copies, 'row', 0, 0, tiled=True)]
    ppermute x5 -> x0, waiting for transfers between devices: 21 us -> none  [body(): lax.ppermute(col_local, 'row', [(i, i ^ step) for i in range(n_row)])]
    all_to_all x0 -> x1, waiting for transfers between devices: none -> 14.9 us  [body(): dst_recv = lax.all_to_all(dst_copies, 'row', 0, 0, tiled=True)]
    all_to_all x0 -> x1, starting transfers between devices: none -> 13.4 us  [body(): dst_recv = lax.all_to_all(dst_copies, 'row', 0, 0, tiled=True)]
    ppermute x5 -> x0, starting transfers between devices: 13.4 us -> none  [body(): lax.ppermute(col_local, 'row', [(i, i ^ step) for i in range(n_row)])]
    all_to_all x1, waiting for transfers between devices: 0.01 us -> 12.4 us  [body(): recv = lax.all_to_all(send, 'col', 0, 0, tiled=True)]
    all_gather x1, blocking collectives: 18 us -> 15 us  [body(): row_all = lax.all_gather(row_local, 'col', axis=0, tiled=False)]
  transfers between devices with their start and end apart: 6 -> 2, of which waited for: 5 -> 2; matrix products, arithmetic and copies ran while one was open for 4% -> 3% of each run, Pallas kernels for 0% -> 0%
where the time goes in v2:
time: 146 us; the launch traced here: 144 us
  blocking collectives  37.7 us (26%)
  Pallas kernels  35.1 us (24%)
  waiting for transfers between devices  27.3 us (19%)
  starting transfers between devices  20.6 us (14%)
  other arithmetic  12.4 us (8%)
  local copies, waits for them, and re-layouts  10 us (7%)
    pallas_call x2, Pallas kernels, tile_lse(): pl.pallas_call(tile_kernel, grid=(slots, n_cc), in_specs=[pl.BlockSpec((1...  35.1 us
    all_to_all x1, blocking collectives, body(): col_all = lax.all_to_all(col_copies, 'row', 0, 0, tiled=True)  22.7 us
    all_gather x1, blocking collectives, body(): row_all = lax.all_gather(row_local, 'col', axis=0, tiled=False)  15 us
    all_to_all x1, waiting for transfers between devices, body(): dst_recv = lax.all_to_all(dst_copies, 'row', 0, 0, tiled=True)  14.9 us
    all_to_all x1, starting transfers between devices, body(): dst_recv = lax.all_to_all(dst_copies, 'row', 0, 0, tiled=True)  13.4 us
    all_to_all x1, waiting for transfers between devices, body(): recv = lax.all_to_all(send, 'col', 0, 0, tiled=True)  12.4 us
    all_to_all x1, starting transfers between devices, body(): recv = lax.all_to_all(send, 'col', 0, 0, tiled=True)  7.21 us
  transfers between devices with their start and end apart: 2, of which 2 were waited for; matrix products, arithmetic and copies ran while one was open for 3% of the time, Pallas kernels for 0%

profile of v2, /device:TPU:6, one launch (start us, length us, event | category | flops | bytes accessed | tf_op | source)
XLA Modules:
  0.0 144.0 jit_solution(12483870559796808180)
XLA Ops:
  0.7 0.8 add_select_fusion.1
  1.5 0.1 fusion
  1.8 0.2 select_reduce_fusion.2
  2.1 0.1 reshape.311
  2.2 0.1 copy.91
  2.3 0.9 gather_fusion.1
  3.2 1.0 broadcast_select_fusion
  4.2 7.2 %all-to-all-start.1 = ((bf16[16,3,4,1024]{3,2,1,0:T(4,128)(2,1)}), bf16[16,3,4,1024]{3,2,1,0:T(4,128)(2,1)S(1)}, u32[]{:S(2)}, u32[]{:S(2)}) async-start(bf16[16,3,4,1024]{3,2,1,0:T(4,128)(2,1)} %broadcast_select_fusion), calls=%async_computation.1 | async-start | bytes 786432 | tf_op jit(solution)/shard_map/all_to_all | solution.py:102
  11.5 0.2 dynamic-slice_reduce_fusion
  11.7 0.6 gather_fusion
  12.2 0.1 fusion.11
  12.5 0.1 fusion.19
  12.6 12.4 %all-to-all-done.1 = bf16[16,3,4,1024]{3,2,1,0:T(4,128)(2,1)S(1)} async-done(((bf16[16,3,4,1024]{3,2,1,0:T(4,128)(2,1)}), bf16[16,3,4,1024]{3,2,1,0:T(4,128)(2,1)S(1)}, u32[]{:S(2)}, u32[]{:S(2)}) %all-to-all-start.1) | async-done | bytes 393248 | tf_op jit(solution)/shard_map/all_to_all | solution.py:102
  25.0 1.3 broadcast_in_dim.156
  26.3 13.4 %all-to-all-start = ((bf16[32,4,2,1024]{3,2,1,0:T(2,128)(2,1)}), bf16[32,4,2,1024]{3,2,1,0:T(2,128)(2,1)S(1)}, u32[]{:S(2)}, u32[]{:S(2)}) async-start(bf16[32,4,2,1024]{3,2,1,0:T(2,128)(2,1)} %broadcast_in_dim.156), calls=%async_computation | async-start | bytes 1048576 | tf_op jit(solution)/shard_map/all_to_all | solution.py:83
  39.7 0.2 dynamic-slice_reduce_fusion.1
  39.9 0.2 compare_reduce_fusion
  40.1 0.2 fusion.18
  40.3 0.2 copy.93
  40.5 0.1 reshape.312.rhs_ref
  40.6 0.2 multiply_reduce_fusion.1
  40.9 0.5 copy.101
  41.4 0.4 copy.97
  41.7 1.0 multiply_bitcast_fusion.lhs_ref
  42.7 14.9 %all-to-all-done = bf16[32,4,2,1024]{3,2,1,0:T(2,128)(2,1)S(1)} async-done(((bf16[32,4,2,1024]{3,2,1,0:T(2,128)(2,1)}), bf16[32,4,2,1024]{3,2,1,0:T(2,128)(2,1)S(1)}, u32[]{:S(2)}, u32[]{:S(2)}) %all-to-all-start) | async-done | bytes 524320 | tf_op jit(solution)/shard_map/all_to_all | solution.py:83
  57.6 0.4 copy.90
  58.0 0.2 reshape.310.rhs_ref
  58.3 1.3 copy.94.lhs_ref
  59.6 0.6 multiply_reduce_fusion
  60.2 2.0 %copy.95.bias_ref = f32[4,1024,1]{2,1,0:T(8,128)} copy(f32[4,1024,1]{1,0,2:T(4,128)S(1)} %subtract_bitcast_fusion) | data formatting | bytes 32768 | tf_op jit(solution)/shard_map/broadcast_in_dim | solution.py:120
  62.2 17.5 %shard_map.77 = f32[3,4,1,1024]{3,2,1,0:T(1,128)} custom-call(bf16[4,1024,64]{2,1,0:T(8,128)(2,1)} %copy.94.lhs_ref, f32[4,1024,1]{2,1,0:T(8,128)} %copy.95.bias_ref, bf16[3,64,1024]{2,1,0:T(8,128)(2,1)} %copy-done.2), custom_call_target="tpu_custom_call" | custom-call | tf_op jit(solution)/shard_map/pallas_call | solution.py:51
  79.7 0.9 fusion.5
  80.7 0.9 fusion.8
  81.7 15.0 %all_gather.4 = f32[16,3,1024]{2,1,0:T(4,128)S(1)} all-gather(f32[1,3,1024]{2,1,0:T(4,128)S(1)} %fusion.12), channel_id=1, replica_groups=mesh['row'=32,'col'=16] {'col'}, dimensions={0}, use_global_device_ids=true | all-gather | bytes 208896 | tf_op jit(solution)/shard_map/all_gather | solution.py:125
  96.7 0.1 copy.96
  96.8 0.7 select_reduce_fusion.1
  97.5 0.8 select_reduce_fusion
  98.4 0.6 gather_fusion.2
  99.0 0.5 copy.99
  99.5 1.4 multiply_subtract_fusion.bias_ref
  100.9 17.5 %shard_map.78 = f32[3,4,1,1024]{3,2,1,0:T(1,128)} custom-call(bf16[3,1024,64]{2,1,0:T(8,128)(2,1)} %multiply_bitcast_fusion.lhs_ref, f32[3,1024,1]{2,1,0:T(8,128)} %multiply_subtract_fusion.bias_ref, bf16[4,64,1024]{2,1,0:T(8,128)(2,1)} %copy-done.1), custom_call_target="tpu_custom_call" | custom-call | tf_op jit(solution)/shard_map/pallas_call | solution.py:51
  118.4 0.9 fusion.1
  119.3 0.9 fusion.4
  120.3 0.1 broadcast_in_dim.171
  120.4 22.7 %all_to_all.15 = f32[32,4,1024]{2,1,0:T(4,128)S(1)} all-to-all(f32[32,4,1024]{2,1,0:T(4,128)S(1)} %broadcast_in_dim.171), channel_id=1, replica_groups=mesh['row'=32,'col'=16] {'row'}, dimensions={0} | all-to-all | bytes 1048576 | tf_op jit(solution)/shard_map/all_to_all | solution.py:141
  143.1 0.1 reduce_max.39
  143.2 0.2 exponential_reduce_fusion
  143.4 0.6 subtract_multiply_fusion.1
  (41 shorter events, 0.9 us)
Async XLA Ops:
  0.6 1.7 %copy-start = (bf16[16,4,1024]{2,1,0:T(4,128)(2,1)S(1)}, bf16[16,4,1024]{2,1,0:T(4,128)(2,1)}, u32[]{:S(2)}) copy-start(bf16[16,4,1024]{2,1,0:T(4,128)(2,1)} %param.6) | copy-start | bytes 393220
  0.6 10.8 %copy-start.8 = (s32[16,8]{0,1:T(8,128)S(1)}, s32[16,8]{0,1:T(8,128)}, u32[]{:S(2)}) copy-start(s32[16,8]{0,1:T(8,128)} %param.8) | copy-start | bytes 1540
  0.7 24.4 %copy-start.5 = (bf16[4,2,1024]{2,1,0:T(2,128)(2,1)S(1)}, bf16[4,2,1024]{2,1,0:T(2,128)(2,1)}, u32[]{:S(2)}) copy-start(bf16[4,2,1024]{2,1,0:T(2,128)(2,1)} %param.7) | copy-start | bytes 49156
  4.2 20.8 %all-to-all-start.1 = ((bf16[16,3,4,1024]{3,2,1,0:T(4,128)(2,1)}), bf16[16,3,4,1024]{3,2,1,0:T(4,128)(2,1)S(1)}, u32[]{:S(2)}, u32[]{:S(2)}) async-start(bf16[16,3,4,1024]{3,2,1,0:T(4,128)(2,1)} %broadcast_select_fusion), calls=%async_computation.1 | async-start | bytes 786432 | tf_op jit(solution)/shard_map/all_to_all | solution.py:102
  26.3 31.3 %all-to-all-start = ((bf16[32,4,2,1024]{3,2,1,0:T(2,128)(2,1)}), bf16[32,4,2,1024]{3,2,1,0:T(2,128)(2,1)S(1)}, u32[]{:S(2)}, u32[]{:S(2)}) async-start(bf16[32,4,2,1024]{3,2,1,0:T(2,128)(2,1)} %broadcast_in_dim.156), calls=%async_computation | async-start | bytes 1048576 | tf_op jit(solution)/shard_map/all_to_all | solution.py:83
  40.6 2.1 %copy-start.2 = (bf16[3,64,1024]{2,1,0:T(8,128)(2,1)}, bf16[3,64,1024]{2,1,0:T(8,128)(2,1)S(1)}, u32[]{:S(2)}) copy-start(bf16[3,64,1024]{2,1,0:T(8,128)(2,1)S(1)} %reshape.312.rhs_ref) | copy-start | bytes 1179652
  58.0 2.2 %copy-start.6 = (f32[4,1024]{1,0:T(4,128)S(1)}, f32[4,1024]{1,0:T(4,128)}, u32[]{:S(2)}) copy-start(f32[4,1024]{1,0:T(4,128)} %param.11) | copy-start | bytes 49156
  58.2 4.0 %copy-start.1 = (bf16[4,64,1024]{2,1,0:T(8,128)(2,1)}, bf16[4,64,1024]{2,1,0:T(8,128)(2,1)S(1)}, u32[]{:S(2)}) copy-start(bf16[4,64,1024]{2,1,0:T(8,128)(2,1)S(1)} %reshape.310.rhs_ref) | copy-start | bytes 1572868
  79.7 18.6 %copy-start.4 = (f32[16,1024]{1,0:T(8,128)S(1)}, f32[16,1024]{1,0:T(8,128)}, u32[]{:S(2)}) copy-start(f32[16,1024]{1,0:T(8,128)} %param.9) | copy-start | bytes 196612
  98.4 2.5 %copy-start.3 = (f32[16,1024]{1,0:T(8,128)}, f32[16,1024]{1,0:T(8,128)S(1)}, u32[]{:S(2)}) copy-start(f32[16,1024]{1,0:T(8,128)S(1)} %subtract_multiply_fusion) | copy-start | bytes 196612
  118.4 25.0 %copy-start.7 = (f32[4,1024]{1,0:T(4,128)S(1)}, f32[4,1024]{1,0:T(4,128)}, u32[]{:S(2)}) copy-start(f32[4,1024]{1,0:T(4,128)} %param.10) | copy-start | bytes 49156

commit v3 on v2

--- a/solution.py
+++ b/solution.py
@@ -14,15 +14,17 @@
 
 
 def tile_kernel(lhs_ref, bias_ref, rhs_ref, out_ref):
-    reduced = lhs_ref.shape[1]
+    reduced = lhs_ref.shape[2]
     kept = rhs_ref.shape[2]
     rhs = rhs_ref[0]
 
     def chunk(ci, carry):
         high, total = carry
         start = pl.multiple_of(ci * CHUNK, CHUNK)
-        left = lhs_ref[0, pl.ds(start, CHUNK), :]
-        vals = jnp.dot(left, rhs, preferred_element_type=jnp.float32)
+        left = lhs_ref[0, :, pl.ds(start, CHUNK)]
+        vals = lax.dot_general(
+            left, rhs, (((0,), (0,)), ((), ())), preferred_element_type=jnp.float32
+        )
         vals = vals + bias_ref[0, pl.ds(start, CHUNK), :]
         new_high = jnp.maximum(high, jnp.max(vals, axis=0, keepdims=True))
         total = total * jnp.exp(high - new_high) + jnp.sum(
@@ -39,7 +41,7 @@
 
 
 def tile_lse(lhs, bias, rhs, lhs_by_slot):
-    n_lhs, reduced, depth = lhs.shape
+    n_lhs, depth, reduced = lhs.shape
     n_rhs, _, kept = rhs.shape
     slots, n_cc = (n_lhs, n_rhs) if lhs_by_slot else (n_rhs, n_lhs)
     if lhs_by_slot:
@@ -52,7 +54,7 @@
         tile_kernel,
         grid=(slots, n_cc),
         in_specs=[
-            pl.BlockSpec((1, reduced, depth), lhs_map),
+            pl.BlockSpec((1, depth, reduced), lhs_map),
             pl.BlockSpec((1, reduced, 1), lhs_map),
             pl.BlockSpec((1, depth, kept), rhs_map),
         ],
@@ -81,7 +83,6 @@
 
     dst_copies = jnp.broadcast_to(dst_points[None], (n_row,) + dst_points.shape)
     dst_recv = lax.all_to_all(dst_copies, "row", 0, 0, tiled=True)
-    dst_full = dst_recv.transpose(1, 0, 2, 3).reshape(col_count, -1, dst_points.shape[2])
 
     dev_of = support // col_count
     touches = jnp.any(
@@ -96,12 +97,14 @@
     )
     slot_ok = jnp.any(onehot, axis=2)
 
+    dst_recv, src_points = lax.optimization_barrier((dst_recv, src_points))
     send = jnp.take(src_points, table.reshape(-1), axis=0).reshape(
         n_col, SLOTS, dim_part, pts
     )
     recv = lax.all_to_all(send, "col", 0, 0, tiled=True)
     src_mine = recv.transpose(1, 0, 2, 3).reshape(SLOTS, n_col * dim_part, pts)
 
+    dst_full = dst_recv.transpose(1, 0, 2, 3).reshape(col_count, -1, pts)
     my_table = lax.dynamic_index_in_dim(table, col_id, 0, keepdims=False)
     my_ok = lax.dynamic_index_in_dim(slot_ok, col_id, 0, keepdims=False)
     my_support = jnp.take(support, my_table, axis=0)
@@ -116,7 +119,7 @@
     dst_vals = dst_full.astype(jnp.float32)
     dst_sq = jnp.sum(dst_vals * dst_vals, axis=1)
 
-    dst_lhs = (dst_full * 4).transpose(0, 2, 1)
+    dst_lhs = dst_full * 4
     dst_bias = (2.0 * dst_potential - 2.0 * dst_sq)[:, :, None]
     row_tiles = tile_lse(dst_lhs, dst_bias, src_mine, lhs_by_slot=False)[:, :, 0, :]
     row_local = masked_lse(row_tiles, valid[:, :, None], axis=1) - 2.0 * src_sq
@@ -132,7 +135,7 @@
     src_new = blur_scale * (log_src_mass - whole)
 
     my_pot = jnp.take(src_new, my_table, axis=0)
-    src_lhs = (src_mine * 4).transpose(0, 2, 1)
+    src_lhs = src_mine * 4
     src_bias = (2.0 * my_pot - 2.0 * src_sq)[:, :, None]
     col_tiles = tile_lse(src_lhs, src_bias, dst_full, lhs_by_slot=True)[:, :, 0, :]
     col_local = masked_lse(col_tiles, valid[:, :, None], axis=0)

time: 146 us -> 142 us (0.973)
  waiting for transfers between devices: 27.3 us -> 22.3 us
    all_to_all x1, waiting for transfers between devices: 12.4 us -> 9.32 us  [body(): recv = lax.all_to_all(send, 'col', 0, 0, tiled=True)]
    all_to_all x1, waiting for transfers between devices: 14.9 us -> 13 us  [body(): dst_recv = lax.all_to_all(dst_copies, 'row', 0, 0, tiled=True)]
    mul x0 -> x2, other arithmetic: none -> 1.76 us  [the longest x1 0.92 us: body(): dst_lhs = dst_full * 4]
  transfers between devices with their start and end apart: 2 -> 2, of which waited for: 2 -> 2; matrix products, arithmetic and copies ran while one was open for 3% -> 6% of each run, Pallas kernels for 0% -> 0%
where the time goes in v3:
time: 142 us; the launch traced here: 141 us
  blocking collectives  38.8 us (27%)
  Pallas kernels  35.4 us (25%)
  waiting for transfers between devices  22.3 us (16%)
  starting transfers between devices  20.7 us (15%)
  other arithmetic  13.1 us (9%)
  local copies, waits for them, and re-layouts  9.75 us (7%)
    pallas_call x2, Pallas kernels, tile_lse(): pl.pallas_call(tile_kernel, grid=(slots, n_cc), in_specs=[pl.BlockSpec((1...  35.4 us
    all_to_all x1, blocking collectives, body(): col_all = lax.all_to_all(col_copies, 'row', 0, 0, tiled=True)  22.7 us
    all_gather x1, blocking collectives, body(): row_all = lax.all_gather(row_local, 'col', axis=0, tiled=False)  16.1 us
    all_to_all x1, starting transfers between devices, body(): dst_recv = lax.all_to_all(dst_copies, 'row', 0, 0, tiled=True)  13.5 us
    all_to_all x1, waiting for transfers between devices, body(): dst_recv = lax.all_to_all(dst_copies, 'row', 0, 0, tiled=True)  13 us
    all_to_all x1, waiting for transfers between devices, body(): recv = lax.all_to_all(send, 'col', 0, 0, tiled=True)  9.32 us
    all_to_all x1, starting transfers between devices, body(): recv = lax.all_to_all(send, 'col', 0, 0, tiled=True)  7.21 us
  transfers between devices with their start and end apart: 2, of which 2 were waited for; matrix products, arithmetic and copies ran while one was open for 6% of the time, Pallas kernels for 0%

profile of v3, /device:TPU:6, one launch (start us, length us, event | category | flops | bytes accessed | tf_op | source)
XLA Modules:
  0.0 140.9 jit_solution(3182362619380983970)
XLA Ops:
  0.6 2.0 %broadcast_in_dim.156 = bf16[32,4,2,1024]{3,2,1,0:T(2,128)(2,1)} broadcast(bf16[4,2,1024]{2,1,0:T(2,128)(2,1)} %param.7), dimensions={1,2,3} | broadcast | bytes 540672 | tf_op jit(solution)/shard_map/broadcast_in_dim | solution.py:84
  2.7 13.5 %all-to-all-start = ((bf16[32,4,2,1024]{3,2,1,0:T(2,128)(2,1)}), bf16[32,4,2,1024]{3,2,1,0:T(2,128)(2,1)S(1)}, u32[]{:S(2)}, u32[]{:S(2)}) async-start(bf16[32,4,2,1024]{3,2,1,0:T(2,128)(2,1)} %broadcast_in_dim.156), calls=%async_computation | async-start | bytes 1048576 | tf_op jit(solution)/shard_map/all_to_all | solution.py:85
  16.2 0.7 add_select_fusion.1
  17.0 0.1 fusion
  17.3 0.2 select_reduce_fusion.2
  17.5 0.2 fusion.11
  17.7 0.2 dynamic-slice_reduce_fusion
  17.9 0.1 reshape.311
  18.0 0.8 copy.77
  18.8 0.2 dynamic-slice_reduce_fusion.1
  19.0 0.1 copy.79
  19.1 0.6 gather_fusion
  19.7 0.2 compare_reduce_fusion
  19.9 0.1 fusion.19
  20.1 13.0 %all-to-all-done = bf16[32,4,2,1024]{3,2,1,0:T(2,128)(2,1)S(1)} async-done(((bf16[32,4,2,1024]{3,2,1,0:T(2,128)(2,1)}), bf16[32,4,2,1024]{3,2,1,0:T(2,128)(2,1)S(1)}, u32[]{:S(2)}, u32[]{:S(2)}) %all-to-all-start) | async-done | bytes 524320 | tf_op jit(solution)/shard_map/all_to_all | solution.py:85
  33.0 0.9 gather_fusion.1
  33.9 1.0 broadcast_select_fusion
  34.9 7.2 %all-to-all-start.1 = ((bf16[16,3,4,1024]{3,2,1,0:T(4,128)(2,1)}), bf16[16,3,4,1024]{3,2,1,0:T(4,128)(2,1)S(1)}, u32[]{:S(2)}, u32[]{:S(2)}) async-start(bf16[16,3,4,1024]{3,2,1,0:T(4,128)(2,1)} %broadcast_select_fusion), calls=%async_computation.1 | async-start | bytes 786432 | tf_op jit(solution)/shard_map/all_to_all | solution.py:104
  42.2 0.2 fusion.18
  42.4 0.6 multiply_reduce_fusion
  43.0 2.0 %copy.82.bias_ref = f32[4,1024,1]{2,1,0:T(8,128)} copy(f32[4,1024,1]{1,0,2:T(4,128)S(1)} %subtract_bitcast_fusion) | data formatting | bytes 32768 | tf_op jit(solution)/shard_map/broadcast_in_dim | solution.py:123
  45.0 0.4 copy.78
  45.3 0.2 reshape.310.rhs_ref
  45.6 0.9 broadcast_multiply_fusion.lhs_ref
  46.5 9.3 %all-to-all-done.1 = bf16[16,3,4,1024]{3,2,1,0:T(4,128)(2,1)S(1)} async-done(((bf16[16,3,4,1024]{3,2,1,0:T(4,128)(2,1)}), bf16[16,3,4,1024]{3,2,1,0:T(4,128)(2,1)S(1)}, u32[]{:S(2)}, u32[]{:S(2)}) %all-to-all-start.1) | async-done | bytes 393248 | tf_op jit(solution)/shard_map/all_to_all | solution.py:104
  55.8 0.1 copy.81
  55.9 0.1 reshape.312.rhs_ref
  56.1 0.8 broadcast_multiply_fusion.1.lhs_ref
  56.9 17.7 %shard_map.77 = f32[3,4,1,1024]{3,2,1,0:T(1,128)} custom-call(bf16[4,64,1024]{2,1,0:T(8,128)(2,1)} %broadcast_multiply_fusion.lhs_ref, f32[4,1024,1]{2,1,0:T(8,128)} %copy.82.bias_ref, bf16[3,64,1024]{2,1,0:T(8,128)(2,1)} %copy-done.2), custom_call_target="tpu_custom_call" | custom-call | tf_op jit(solution)/shard_map/pallas_call | solution.py:53
  74.6 0.9 fusion.5
  75.6 0.9 fusion.8
  76.5 0.2 multiply_reduce_fusion.1
  76.8 16.1 %all_gather.4 = f32[16,3,1024]{2,1,0:T(4,128)S(1)} all-gather(f32[1,3,1024]{2,1,0:T(4,128)S(1)} %fusion.12), channel_id=1, replica_groups=mesh['row'=32,'col'=16] {'col'}, dimensions={0}, use_global_device_ids=true | all-gather | bytes 208896 | tf_op jit(solution)/shard_map/all_gather | solution.py:128
  92.9 0.1 copy.83
  93.0 0.7 select_reduce_fusion.1
  93.7 0.8 select_reduce_fusion
  94.6 0.6 gather_fusion.2
  95.2 0.5 copy.84
  95.7 0.5 copy.86
  96.2 1.4 multiply_subtract_fusion.bias_ref
  97.6 17.7 %shard_map.78 = f32[3,4,1,1024]{3,2,1,0:T(1,128)} custom-call(bf16[3,64,1024]{2,1,0:T(8,128)(2,1)} %broadcast_multiply_fusion.1.lhs_ref, f32[3,1024,1]{2,1,0:T(8,128)} %multiply_subtract_fusion.bias_ref, bf16[4,64,1024]{2,1,0:T(8,128)(2,1)} %copy-done.1), custom_call_target="tpu_custom_call" | custom-call | tf_op jit(solution)/shard_map/pallas_call | solution.py:53
  115.3 0.9 fusion.1
  116.2 0.9 fusion.4
  117.2 0.1 broadcast_in_dim.171
  117.3 22.7 %all_to_all.15 = f32[32,4,1024]{2,1,0:T(4,128)S(1)} all-to-all(f32[32,4,1024]{2,1,0:T(4,128)S(1)} %broadcast_in_dim.171), channel_id=1, replica_groups=mesh['row'=32,'col'=16] {'row'}, dimensions={0} | all-to-all | bytes 1048576 | tf_op jit(solution)/shard_map/all_to_all | solution.py:144
  140.0 0.1 reduce_max.39
  140.1 0.2 exponential_reduce_fusion
  140.3 0.6 subtract_multiply_fusion.1
  (35 shorter events, 0.8 us)
Async XLA Ops:
  0.6 32.4 %copy-start = (bf16[16,4,1024]{2,1,0:T(4,128)(2,1)S(1)}, bf16[16,4,1024]{2,1,0:T(4,128)(2,1)}, u32[]{:S(2)}) copy-start(bf16[16,4,1024]{2,1,0:T(4,128)(2,1)} %param.6) | copy-start | bytes 393220
  2.7 40.3 %copy-start.5 = (f32[4,1024]{1,0:T(4,128)S(1)}, f32[4,1024]{1,0:T(4,128)}, u32[]{:S(2)}) copy-start(f32[4,1024]{1,0:T(4,128)} %param.11) | copy-start | bytes 49156
  2.7 30.4 %all-to-all-start = ((bf16[32,4,2,1024]{3,2,1,0:T(2,128)(2,1)}), bf16[32,4,2,1024]{3,2,1,0:T(2,128)(2,1)S(1)}, u32[]{:S(2)}, u32[]{:S(2)}) async-start(bf16[32,4,2,1024]{3,2,1,0:T(2,128)(2,1)} %broadcast_in_dim.156), calls=%async_computation | async-start | bytes 1048576 | tf_op jit(solution)/shard_map/all_to_all | solution.py:85
  34.9 20.8 %all-to-all-start.1 = ((bf16[16,3,4,1024]{3,2,1,0:T(4,128)(2,1)}), bf16[16,3,4,1024]{3,2,1,0:T(4,128)(2,1)S(1)}, u32[]{:S(2)}, u32[]{:S(2)}) async-start(bf16[16,3,4,1024]{3,2,1,0:T(4,128)(2,1)} %broadcast_select_fusion), calls=%async_computation.1 | async-start | bytes 786432 | tf_op jit(solution)/shard_map/all_to_all | solution.py:104
  45.6 29.1 %copy-start.1 = (bf16[4,64,1024]{2,1,0:T(8,128)(2,1)}, bf16[4,64,1024]{2,1,0:T(8,128)(2,1)S(1)}, u32[]{:S(2)}) copy-start(bf16[4,64,1024]{2,1,0:T(8,128)(2,1)S(1)} %reshape.310.rhs_ref) | copy-start | bytes 1572868
  56.0 0.9 copy-start.2
  74.6 19.9 %copy-start.4 = (f32[16,1024]{1,0:T(8,128)S(1)}, f32[16,1024]{1,0:T(8,128)}, u32[]{:S(2)}) copy-start(f32[16,1024]{1,0:T(8,128)} %param.9) | copy-start | bytes 196612
  94.6 3.0 %copy-start.3 = (f32[16,1024]{1,0:T(8,128)}, f32[16,1024]{1,0:T(8,128)S(1)}, u32[]{:S(2)}) copy-start(f32[16,1024]{1,0:T(8,128)S(1)} %subtract_multiply_fusion) | copy-start | bytes 196612
  97.6 42.7 %copy-start.6 = (f32[4,1024]{1,0:T(4,128)S(1)}, f32[4,1024]{1,0:T(4,128)}, u32[]{:S(2)}) copy-start(f32[4,1024]{1,0:T(4,128)} %param.10) | copy-start | bytes 49156

commit v4 on v3

v4 whole, which is shorter than its diff:
```python
import functools

import jax
import jax.numpy as jnp
from jax import lax
from jax.experimental import pallas as pl
from jax.experimental.pallas import tpu as pltpu
from jax.sharding import PartitionSpec as P

blur_scale = 0.5
floor_value = -1e30
SLOTS = 3
CHUNK = 256


def tile_kernel(valid_ref, lhs_ref, bias_ref, rhs_ref, sub_ref, out_ref, acc_high, acc_total):
    outer = pl.program_id(0)
    inner = pl.program_id(1)
    n_inner = pl.num_programs(1)
    reduced = lhs_ref.shape[2]
    kept = rhs_ref.shape[2]

    @pl.when(inner == 0)
    def _():
        acc_high[...] = jnp.full((1, kept), floor_value, jnp.float32)
        acc_total[...] = jnp.zeros((1, kept), jnp.float32)

    @pl.when(valid_ref[outer * n_inner + inner] > 0)
    def _():
        rhs = rhs_ref[0]

        def chunk(ci, carry):
            high, total = carry
            start = pl.multiple_of(ci * CHUNK, CHUNK)
            left = lhs_ref[0, :, pl.ds(start, CHUNK)]
            vals = lax.dot_general(
                left, rhs, (((0,), (0,)), ((), ())), preferred_element_type=jnp.float32
            )
            vals = vals + bias_ref[0, pl.ds(start, CHUNK), :]
            new_high = jnp.maximum(high, jnp.max(vals, axis=0, keepdims=True))
            total = total * jnp.exp(high - new_high) + jnp.sum(
                jnp.exp(vals - new_high), axis=0, keepdims=True
            )
            return new_high, total

        start = (
            jnp.full((1, kept), floor_value, jnp.float32),
            jnp.zeros((1, kept), jnp.float32),
        )
        high, total = lax.fori_loop(0, reduced // CHUNK, chunk, start, unroll=True)
        old_high = acc_high[...]
        new_high = jnp.maximum(old_high, high)
        acc_total[...] = acc_total[...] * jnp.exp(old_high - new_high) + total * jnp.exp(
            high - new_high
        )
        acc_high[...] = new_high

    @pl.when(inner == n_inner - 1)
    def _():
        total = acc_total[...]
        found = total > 0.0
        whole = acc_high[...] + jnp.log(jnp.where(found, total, 1.0))
        out_ref[0] = jnp.where(found, whole - sub_ref[0], floor_value)


def tile_lse(valid, lhs, bias, rhs, sub):
    n_in, depth, reduced = lhs.shape
    n_out, _, kept = rhs.shape
    grid_spec = pltpu.PrefetchScalarGridSpec(
        num_scalar_prefetch=1,
        grid=(n_out, n_in),
        in_specs=[
            pl.BlockSpec((1, depth, reduced), lambda o, n, v: (n, 0, 0)),
            pl.BlockSpec((1, reduced, 1), lambda o, n, v: (n, 0, 0)),
            pl.BlockSpec((1, depth, kept), lambda o, n, v: (o, 0, 0)),
            pl.BlockSpec((1, 1, kept), lambda o, n, v: (o, 0, 0)),
        ],
        out_specs=pl.BlockSpec((1, 1, kept), lambda o, n, v: (o, 0, 0)),
        scratch_shapes=[pltpu.VMEM((1, kept), jnp.float32), pltpu.VMEM((1, kept), jnp.float32)],
    )
    return pl.pallas_call(
        tile_kernel,
        grid_spec=grid_spec,
        out_shape=jax.ShapeDtypeStruct((n_out, 1, kept), jnp.float32),
    )(valid, lhs, bias, rhs, sub)


def masked_lse(values, mask, axis):
    high = jnp.max(jnp.where(mask, values, floor_value), axis=axis)
    total = jnp.sum(
        jnp.where(mask, jnp.exp(values - jnp.expand_dims(high, axis)), 0.0), axis=axis
    )
    return jnp.where(jnp.any(mask, axis=axis), high + jnp.log(total), floor_value)


def log_add(first, second):
    high = jnp.maximum(first, second)
    return high + jnp.log(jnp.exp(first - high) + jnp.exp(second - high))


def body(src_points, dst_points, support, log_src_mass, log_dst_mass, dst_potential, n_row, n_col):
    row_count, dim_part, pts = src_points.shape
    col_count = dst_points.shape[0]
    col_id = lax.axis_index("col")

    dst_copies = jnp.broadcast_to(dst_points[None], (n_row,) + dst_points.shape)
    dst_recv = lax.all_to_all(dst_copies, "row", 0, 0, tiled=True)

    dev_of = support // col_count
    touches = jnp.any(
        dev_of[:, :, None] == jnp.arange(n_col, dtype=jnp.int32)[None, None, :], axis=1
    )
    rank = jnp.cumsum(touches.astype(jnp.int32), axis=0) - 1
    onehot = touches.T[:, None, :] & (
        rank.T[:, None, :] == jnp.arange(SLOTS, dtype=jnp.int32)[None, :, None]
    )
    table = jnp.sum(
        onehot.astype(jnp.int32) * jnp.arange(row_count, dtype=jnp.int32)[None, None, :], axis=2
    )
    slot_ok = jnp.any(onehot, axis=2)

    send = jnp.take(src_points, table.reshape(-1), axis=0).reshape(
        n_col, SLOTS, dim_part, pts
    ) * 4
    dst_recv, send = lax.optimization_barrier((dst_recv, send))
    recv = lax.all_to_all(send, "col", 0, 0, tiled=True)
    src_four = recv.transpose(1, 0, 2, 3).reshape(SLOTS, n_col * dim_part, pts)

    dst_full = dst_recv.transpose(1, 0, 2, 3).reshape(col_count, -1, pts)
    my_table = lax.dynamic_index_in_dim(table, col_id, 0, keepdims=False)
    my_ok = lax.dynamic_index_in_dim(slot_ok, col_id, 0, keepdims=False)
    my_support = jnp.take(support, my_table, axis=0)
    valid = my_ok[:, None] & jnp.any(
        my_support[:, None, :]
        == (col_id * col_count + jnp.arange(col_count, dtype=jnp.int32))[None, :, None],
        axis=2,
    )

    src_vals = src_four.astype(jnp.float32)
    src_sq = jnp.sum(src_vals * src_vals, axis=1) / 16.0
    dst_vals = dst_full.astype(jnp.float32)
    dst_sq = jnp.sum(dst_vals * dst_vals, axis=1)

    valid_int = valid.astype(jnp.int32)
    dst_bias = (2.0 * dst_potential - 2.0 * dst_sq)[:, :, None]
    row_local = tile_lse(
        valid_int.reshape(-1), dst_full, dst_bias, src_four, (2.0 * src_sq)[:, None, :]
    )[:, 0, :]
    row_local = jnp.where(my_ok[:, None], row_local, floor_value)

    row_all = lax.all_gather(row_local, "col", axis=0, tiled=False)
    owner = onehot.transpose(2, 0, 1)
    whole = masked_lse(
        jnp.broadcast_to(row_all[None], (row_count, n_col, SLOTS, pts)).reshape(row_count, n_col * SLOTS, pts),
        owner.reshape(row_count, n_col * SLOTS)[:, :, None],
        axis=1,
    )
    src_new = blur_scale * (log_src_mass - whole)

    my_pot = jnp.take(src_new, my_table, axis=0)
    src_bias = (2.0 * my_pot - 2.0 * src_sq)[:, :, None]
    col_local = tile_lse(
        valid_int.T.reshape(-1), src_four, src_bias, dst_full, (2.0 * dst_sq)[:, None, :]
    )[:, 0, :]

    col_copies = jnp.broadcast_to(col_local[None], (n_row,) + col_local.shape)
    col_all = lax.all_to_all(col_copies, "row", 0, 0, tiled=True)
    col_high = jnp.max(col_all, axis=0)
    col_whole = col_high + jnp.log(jnp.sum(jnp.exp(col_all - col_high[None]), axis=0))
    dst_new = blur_scale * (log_dst_mass - col_whole)
    return (src_new, dst_new)


def solution(mesh):
    n_row = mesh.shape["row"]
    n_col = mesh.shape["col"]
    return jax.shard_map(
        functools.partial(body, n_row=n_row, n_col=n_col),
        mesh=mesh,
        in_specs=(
            P("row", "col", None),
            P("col", "row", None),
            P("row", None),
            P("row", None),
            P("col", None),
            P("col", None),
        ),
        out_specs=(P("row", None), P("col", None)),
        check_vma=False,
    )
```

time: 142 us -> 139 us (0.979)
  other arithmetic: 13.1 us -> 8.24 us
  local copies, waits for them, and re-layouts: 9.75 us -> 14.5 us
  waiting for transfers between devices: 22.3 us -> 18.7 us
    reduce_max x3 -> x1, other arithmetic: 2.5 us -> 0.67 us  [masked_lse(): high = jnp.max(jnp.where(mask, values, floor_value), axis=axis)]
    all_to_all x1, waiting for transfers between devices: 13 us -> 11.1 us  [body(): dst_recv = lax.all_to_all(dst_copies, 'row', 0, 0, tiled=True)]
    reduce_sum x3 -> x1, other arithmetic: 2.61 us -> 0.81 us  [masked_lse(): jnp.sum(jnp.where(mask, jnp.exp(values - jnp.expand_dims(high, axis)), 0....]
    all_to_all x1, waiting for transfers between devices: 9.32 us -> 7.54 us  [body(): recv = lax.all_to_all(send, 'col', 0, 0, tiled=True)]
    reshape x1 -> x3, local copies, waits for them, and re-layouts: 0.09 us -> 1.54 us  [the longest x1 0.84 us: body(): src_four = recv.transpose(1, 0, 2, 3).reshape(SLOTS, n_col * dim_part, pts)]
  transfers between devices with their start and end apart: 2 -> 2, of which waited for: 2 -> 2; matrix products, arithmetic and copies ran while one was open for 6% -> 8% of each run, Pallas kernels for 0% -> 0%
where the time goes in v4:
time: 139 us; the launch traced here: 138 us
  blocking collectives  38.8 us (28%)
  Pallas kernels  36.2 us (26%)
  starting transfers between devices  20.6 us (15%)
  waiting for transfers between devices  18.7 us (13%)
  local copies, waits for them, and re-layouts  14.5 us (10%)
  other arithmetic  8.24 us (6%)
    pallas_call x2, Pallas kernels, tile_lse(): pl.pallas_call(tile_kernel, grid_spec=grid_spec, out_shape=jax.ShapeDtype...  36.2 us
    all_to_all x1, blocking collectives, body(): col_all = lax.all_to_all(col_copies, 'row', 0, 0, tiled=True)  22.4 us
    all_gather x1, blocking collectives, body(): row_all = lax.all_gather(row_local, 'col', axis=0, tiled=False)  16.4 us
    all_to_all x1, starting transfers between devices, body(): dst_recv = lax.all_to_all(dst_copies, 'row', 0, 0, tiled=True)  13.4 us
    all_to_all x1, waiting for transfers between devices, body(): dst_recv = lax.all_to_all(dst_copies, 'row', 0, 0, tiled=True)  11.1 us
    all_to_all x1, waiting for transfers between devices, body(): recv = lax.all_to_all(send, 'col', 0, 0, tiled=True)  7.54 us
    all_to_all x1, starting transfers between devices, body(): recv = lax.all_to_all(send, 'col', 0, 0, tiled=True)  7.21 us
  transfers between devices with their start and end apart: 2, of which 2 were waited for; matrix products, arithmetic and copies ran while one was open for 8% of the time, Pallas kernels for 0%

profile of v4, /device:TPU:6, one launch (start us, length us, event | category | flops | bytes accessed | tf_op | source)
XLA Modules:
  0.0 137.9 jit_solution(11556062767058127456)
XLA Ops:
  0.6 2.0 %broadcast_in_dim.109 = bf16[32,4,2,1024]{3,2,1,0:T(2,128)(2,1)} broadcast(bf16[4,2,1024]{2,1,0:T(2,128)(2,1)} %param.7), dimensions={1,2,3} | broadcast | bytes 540672 | tf_op jit(solution)/shard_map/broadcast_in_dim | solution.py:106
  2.7 13.4 %all-to-all-start = ((bf16[32,4,2,1024]{3,2,1,0:T(2,128)(2,1)}), bf16[32,4,2,1024]{3,2,1,0:T(2,128)(2,1)S(1)}, u32[]{:S(2)}, u32[]{:S(2)}) async-start(bf16[32,4,2,1024]{3,2,1,0:T(2,128)(2,1)} %broadcast_in_dim.109), calls=%async_computation | async-start | bytes 1048576 | tf_op jit(solution)/shard_map/all_to_all | solution.py:107
  16.1 0.7 add_select_fusion
  16.8 0.8 copy.91
  17.6 0.1 fusion
  17.9 0.2 fusion.3
  18.1 0.2 select_reduce_fusion.2
  18.2 0.1 copy.93
  18.3 0.2 dynamic-slice_reduce_fusion
  18.5 0.2 dynamic-slice_reduce_fusion.1
  18.8 0.1 copy.92
  18.9 0.6 gather_fusion
  19.5 0.9 gather_fusion.1
  20.5 0.2 compare_reduce_fusion
  20.7 1.0 select_multiply_fusion
  21.8 11.1 %all-to-all-done = bf16[32,4,2,1024]{3,2,1,0:T(2,128)(2,1)S(1)} async-done(((bf16[32,4,2,1024]{3,2,1,0:T(2,128)(2,1)}), bf16[32,4,2,1024]{3,2,1,0:T(2,128)(2,1)S(1)}, u32[]{:S(2)}, u32[]{:S(2)}) %all-to-all-start) | async-done | bytes 524320 | tf_op jit(solution)/shard_map/all_to_all | solution.py:107
  32.9 7.2 %all-to-all-start.1 = ((bf16[16,3,4,1024]{3,2,1,0:T(4,128)(2,1)}), bf16[16,3,4,1024]{3,2,1,0:T(4,128)(2,1)S(1)}, u32[]{:S(2)}, u32[]{:S(2)}) async-start(bf16[16,3,4,1024]{3,2,1,0:T(4,128)(2,1)} %select_multiply_fusion), calls=%async_computation.1 | async-start | bytes 786432 | tf_op jit(solution)/shard_map/all_to_all | solution.py:126
  40.2 0.6 reshape.249.valid_ref
  40.8 0.1 fusion.11
  40.9 0.1 copy.99
  41.0 0.6 reshape.251.valid_ref
  41.6 0.4 copy.94
  42.0 1.0 reshape.245.lhs_ref.rhs_ref
  43.0 0.6 multiply_reduce_fusion
  43.6 2.0 %copy.96.bias_ref = f32[4,1024,1]{2,1,0:T(8,128)} copy(f32[4,1024,1]{1,0,2:T(4,128)S(1)} %get-tuple-element.9) | data formatting | bytes 32768 | tf_op jit(solution)/shard_map/broadcast_in_dim | solution.py:145
  45.6 0.6 mul.106.sub_ref
  46.2 7.5 %all-to-all-done.1 = bf16[16,3,4,1024]{3,2,1,0:T(4,128)(2,1)S(1)} async-done(((bf16[16,3,4,1024]{3,2,1,0:T(4,128)(2,1)}), bf16[16,3,4,1024]{3,2,1,0:T(4,128)(2,1)S(1)}, u32[]{:S(2)}, u32[]{:S(2)}) %all-to-all-start.1) | async-done | bytes 393248 | tf_op jit(solution)/shard_map/all_to_all | solution.py:126
  53.8 0.1 copy.95
  53.9 0.8 reshape.246.rhs_ref.lhs_ref
  54.7 0.2 multiply_reduce_fusion.1
  55.0 0.6 mul.101.sub_ref
  55.6 18.0 %shard_map.77 = f32[3,1,1024]{2,1,0:T(1,128)} custom-call(s32[12]{0:T(128)} %reshape.249.valid_ref, bf16[4,64,1024]{2,1,0:T(8,128)(2,1)} %reshape.245.lhs_ref.rhs_ref, f32[4,1024,1]{2,1,0:T(8,128)} %copy.96.bias_ref, bf16[3,64,1024]{2,1,0:T(8,128)(2,1)} %reshape.246.rhs_ref.lhs_ref, f32[3,1,1024]{2,1,0:T(1,128)} %mul.101.sub_ref), custom_call_target="tpu_custom_call" | custom-call | tf_op jit(solution)/shard_map/pallas_call | solution.py:81
  73.6 0.8 broadcast_select_fusion
  74.4 16.4 %all_gather.4 = f32[16,3,1024]{2,1,0:T(4,128)S(1)} all-gather(f32[1,3,1024]{2,1,0:T(4,128)S(1)} %copy.97), channel_id=1, replica_groups=mesh['row'=32,'col'=16] {'col'}, dimensions={0}, use_global_device_ids=true | all-gather | bytes 208896 | tf_op jit(solution)/shard_map/all_gather | solution.py:151
  90.8 0.1 copy.98
  91.0 0.7 select_reduce_fusion.1
  91.6 0.8 select_reduce_fusion
  92.5 0.5 copy.102
  93.1 0.6 gather_fusion.2
  93.6 0.5 copy.100
  94.2 1.4 %multiply_subtract_fusion.bias_ref = f32[3,1024,1]{2,1,0:T(8,128)} fusion(f32[3,1024,1]{2,1,0:T(8,128)S(1)} %copy.102, f32[3,1024,1]{2,1,0:T(8,128)S(1)} %copy.100, pred[3]{0:T(512)(128)(4,1)S(1)} %compare_and_fusion.1), kind=kLoop, calls=%fused_computation.5 | loop fusion | flops 9216 | bytes 36867 | tf_op jit(solution)/shard_map/sub | solution.py:161
  95.6 18.2 %shard_map.78 = f32[4,1,1024]{2,1,0:T(1,128)} custom-call(s32[12]{0:T(128)} %reshape.251.valid_ref, bf16[3,64,1024]{2,1,0:T(8,128)(2,1)} %reshape.246.rhs_ref.lhs_ref, f32[3,1024,1]{2,1,0:T(8,128)} %multiply_subtract_fusion.bias_ref, bf16[4,64,1024]{2,1,0:T(8,128)(2,1)} %reshape.245.lhs_ref.rhs_ref, f32[4,1,1024]{2,1,0:T(1,128)} %mul.106.sub_ref), custom_call_target="tpu_custom_call" | custom-call | tf_op jit(solution)/shard_map/pallas_call | solution.py:81
  113.7 0.7 copy.109
  114.5 0.1 broadcast_in_dim.121
  114.6 22.4 %all_to_all.15 = f32[32,4,1024]{2,1,0:T(4,128)S(1)} all-to-all(f32[32,4,1024]{2,1,0:T(4,128)S(1)} %broadcast_in_dim.121), channel_id=1, replica_groups=mesh['row'=32,'col'=16] {'row'}, dimensions={0} | all-to-all | bytes 1048576 | tf_op jit(solution)/shard_map/all_to_all | solution.py:167
  137.0 0.1 reduce_max.19
  137.1 0.2 exponential_reduce_fusion
  137.2 0.6 subtract_multiply_fusion.1
  (31 shorter events, 0.7 us)
Async XLA Ops:
  0.6 18.9 %copy-start = (bf16[16,4,1024]{2,1,0:T(4,128)(2,1)S(1)}, bf16[16,4,1024]{2,1,0:T(4,128)(2,1)}, u32[]{:S(2)}) copy-start(bf16[16,4,1024]{2,1,0:T(4,128)(2,1)} %param.6) | copy-start | bytes 393220
  2.7 30.2 %all-to-all-start = ((bf16[32,4,2,1024]{3,2,1,0:T(2,128)(2,1)}), bf16[32,4,2,1024]{3,2,1,0:T(2,128)(2,1)S(1)}, u32[]{:S(2)}, u32[]{:S(2)}) async-start(bf16[32,4,2,1024]{3,2,1,0:T(2,128)(2,1)} %broadcast_in_dim.109), calls=%async_computation | async-start | bytes 1048576 | tf_op jit(solution)/shard_map/all_to_all | solution.py:107
  20.7 22.9 %copy-start.3 = (f32[4,1024]{1,0:T(4,128)S(1)}, f32[4,1024]{1,0:T(4,128)}, u32[]{:S(2)}) copy-start(f32[4,1024]{1,0:T(4,128)} %param.11) | copy-start | bytes 49156
  32.9 20.8 %all-to-all-start.1 = ((bf16[16,3,4,1024]{3,2,1,0:T(4,128)(2,1)}), bf16[16,3,4,1024]{3,2,1,0:T(4,128)(2,1)S(1)}, u32[]{:S(2)}, u32[]{:S(2)}) async-start(bf16[16,3,4,1024]{3,2,1,0:T(4,128)(2,1)} %select_multiply_fusion), calls=%async_computation.1 | async-start | bytes 786432 | tf_op jit(solution)/shard_map/all_to_all | solution.py:126
  73.6 19.4 %copy-start.2 = (f32[16,1024]{1,0:T(8,128)S(1)}, f32[16,1024]{1,0:T(8,128)}, u32[]{:S(2)}) copy-start(f32[16,1024]{1,0:T(8,128)} %param.9) | copy-start | bytes 196612
  93.1 2.5 %copy-start.1 = (f32[16,1024]{1,0:T(8,128)}, f32[16,1024]{1,0:T(8,128)S(1)}, u32[]{:S(2)}) copy-start(f32[16,1024]{1,0:T(8,128)S(1)} %subtract_multiply_fusion) | copy-start | bytes 196612
  95.6 41.7 %copy-start.4 = (f32[4,1024]{1,0:T(4,128)S(1)}, f32[4,1024]{1,0:T(4,128)}, u32[]{:S(2)}) copy-start(f32[4,1024]{1,0:T(4,128)} %param.10) | copy-start | bytes 49156

commit v5 on v4

--- a/solution.py
+++ b/solution.py
@@ -36,7 +36,8 @@
             vals = lax.dot_general(
                 left, rhs, (((0,), (0,)), ((), ())), preferred_element_type=jnp.float32
             )
-            vals = vals + bias_ref[0, pl.ds(start, CHUNK), :]
+            bias_row = jnp.broadcast_to(bias_ref[0, :, pl.ds(start, CHUNK)], (8, CHUNK))
+            vals = vals + jnp.transpose(bias_row)[:, 0:1]
             new_high = jnp.maximum(high, jnp.max(vals, axis=0, keepdims=True))
             total = total * jnp.exp(high - new_high) + jnp.sum(
                 jnp.exp(vals - new_high), axis=0, keepdims=True
@@ -71,7 +72,7 @@
         grid=(n_out, n_in),
         in_specs=[
             pl.BlockSpec((1, depth, reduced), lambda o, n, v: (n, 0, 0)),
-            pl.BlockSpec((1, reduced, 1), lambda o, n, v: (n, 0, 0)),
+            pl.BlockSpec((1, 1, reduced), lambda o, n, v: (n, 0, 0)),
             pl.BlockSpec((1, depth, kept), lambda o, n, v: (o, 0, 0)),
             pl.BlockSpec((1, 1, kept), lambda o, n, v: (o, 0, 0)),
         ],
@@ -142,7 +143,7 @@
     dst_sq = jnp.sum(dst_vals * dst_vals, axis=1)
 
     valid_int = valid.astype(jnp.int32)
-    dst_bias = (2.0 * dst_potential - 2.0 * dst_sq)[:, :, None]
+    dst_bias = (2.0 * dst_potential - 2.0 * dst_sq)[:, None, :]
     row_local = tile_lse(
         valid_int.reshape(-1), dst_full, dst_bias, src_four, (2.0 * src_sq)[:, None, :]
     )[:, 0, :]
@@ -157,8 +158,14 @@
     )
     src_new = blur_scale * (log_src_mass - whole)
 
-    my_pot = jnp.take(src_new, my_table, axis=0)
-    src_bias = (2.0 * my_pot - 2.0 * src_sq)[:, :, None]
+    my_owner = jnp.take(owner, my_table, axis=0).reshape(SLOTS, n_col * SLOTS)
+    my_whole = masked_lse(
+        jnp.broadcast_to(row_all.reshape(1, n_col * SLOTS, pts), (SLOTS, n_col * SLOTS, pts)),
+        my_owner[:, :, None],
+        axis=1,
+    )
+    my_pot = blur_scale * (jnp.take(log_src_mass, my_table, axis=0) - my_whole)
+    src_bias = (2.0 * my_pot - 2.0 * src_sq)[:, None, :]
     col_local = tile_lse(
         valid_int.T.reshape(-1), src_four, src_bias, dst_full, (2.0 * dst_sq)[:, None, :]
     )[:, 0, :]

time: 139 us -> 142 us (1.022)
  blocking collectives: 38.8 us -> 17 us
  waiting for transfers between devices: 18.7 us -> 33.7 us
  starting transfers between devices: 20.6 us -> 31.5 us
    all_to_all x1 -> x0, blocking collectives: 22.4 us -> none  [body(): col_all = lax.all_to_all(col_copies, 'row', 0, 0, tiled=True)]
    all_to_all x0 -> x1, waiting for transfers between devices: none -> 14.3 us  [body(): col_all = lax.all_to_all(col_copies, 'row', 0, 0, tiled=True)]
    all_to_all x0 -> x1, starting transfers between devices: none -> 10.7 us  [body(): col_all = lax.all_to_all(col_copies, 'row', 0, 0, tiled=True)]
    all_to_all x1, waiting for transfers between devices: 7.54 us -> 10.1 us  [body(): recv = lax.all_to_all(send, 'col', 0, 0, tiled=True)]
    all_to_all x1, waiting for transfers between devices: 11.1 us -> 9.3 us  [body(): dst_recv = lax.all_to_all(dst_copies, 'row', 0, 0, tiled=True)]
  transfers between devices with their start and end apart: 2 -> 3, of which waited for: 2 -> 3; matrix products, arithmetic and copies ran while one was open for 8% -> 9% of each run, Pallas kernels for 0% -> 0%
where the time goes in v5:
time: 142 us; the launch traced here: 141 us
  Pallas kernels  36.7 us (26%)
  waiting for transfers between devices  33.7 us (24%)
  starting transfers between devices  31.5 us (22%)
  blocking collectives  17 us (12%)
  local copies, waits for them, and re-layouts  13.2 us (9%)
  other arithmetic  8.32 us (6%)
    pallas_call x2, Pallas kernels, tile_lse(): pl.pallas_call(tile_kernel, grid_spec=grid_spec, out_shape=jax.ShapeDtype...  36.7 us
    all_gather x1, blocking collectives, body(): row_all = lax.all_gather(row_local, 'col', axis=0, tiled=False)  17 us
    all_to_all x1, waiting for transfers between devices, body(): col_all = lax.all_to_all(col_copies, 'row', 0, 0, tiled=True)  14.3 us
    all_to_all x1, starting transfers between devices, body(): dst_recv = lax.all_to_all(dst_copies, 'row', 0, 0, tiled=True)  13.5 us
    all_to_all x1, starting transfers between devices, body(): col_all = lax.all_to_all(col_copies, 'row', 0, 0, tiled=True)  10.7 us
    all_to_all x1, waiting for transfers between devices, body(): recv = lax.all_to_all(send, 'col', 0, 0, tiled=True)  10.1 us
    all_to_all x1, waiting for transfers between devices, body(): dst_recv = lax.all_to_all(dst_copies, 'row', 0, 0, tiled=True)  9.3 us
    all_to_all x1, starting transfers between devices, body(): recv = lax.all_to_all(send, 'col', 0, 0, tiled=True)  7.21 us
  transfers between devices with their start and end apart: 3, of which 3 were waited for; matrix products, arithmetic and copies ran while one was open for 9% of the time, Pallas kernels for 0%

profile of v5, /device:TPU:6, one launch (start us, length us, event | category | flops | bytes accessed | tf_op | source)
XLA Modules:
  0.0 141.3 jit_solution(4716059894713264829)
XLA Ops:
  0.6 2.0 %broadcast_in_dim.157 = bf16[32,4,2,1024]{3,2,1,0:T(2,128)(2,1)} broadcast(bf16[4,2,1024]{2,1,0:T(2,128)(2,1)} %param.7), dimensions={1,2,3} | broadcast | bytes 540672 | tf_op jit(solution)/shard_map/broadcast_in_dim | solution.py:107
  2.7 13.5 %all-to-all-start = ((bf16[32,4,2,1024]{3,2,1,0:T(2,128)(2,1)}), bf16[32,4,2,1024]{3,2,1,0:T(2,128)(2,1)S(1)}, u32[]{:S(2)}, u32[]{:S(2)}) async-start(bf16[32,4,2,1024]{3,2,1,0:T(2,128)(2,1)} %broadcast_in_dim.157), calls=%async_computation | async-start | bytes 1048576 | tf_op jit(solution)/shard_map/all_to_all | solution.py:108
  16.4 0.1 fusion
  16.7 0.1 fusion.3
  16.9 0.2 select_reduce_fusion.4
  17.0 0.2 dynamic-slice_reduce_fusion
  17.3 0.4 fusion.12
  17.7 0.2 dynamic-slice_reduce_fusion.1
  18.0 0.6 gather_fusion
  18.6 0.6 gather_fusion.3
  19.2 0.2 compare_reduce_fusion
  19.6 0.7 reshape.296.valid_ref
  20.3 0.6 reshape.294.valid_ref
  20.9 0.1 copy.76
  21.2 0.6 gather_fusion.2
  21.8 0.9 gather_fusion.1
  22.7 1.1 select_multiply_fusion
  23.7 9.3 %all-to-all-done = bf16[32,4,2,1024]{3,2,1,0:T(2,128)(2,1)S(1)} async-done(((bf16[32,4,2,1024]{3,2,1,0:T(2,128)(2,1)}), bf16[32,4,2,1024]{3,2,1,0:T(2,128)(2,1)S(1)}, u32[]{:S(2)}, u32[]{:S(2)}) %all-to-all-start) | async-done | bytes 524320 | tf_op jit(solution)/shard_map/all_to_all | solution.py:108
  33.0 7.2 %all-to-all-start.1 = ((bf16[16,3,4,1024]{3,2,1,0:T(4,128)(2,1)}), bf16[16,3,4,1024]{3,2,1,0:T(4,128)(2,1)S(1)}, u32[]{:S(2)}, u32[]{:S(2)}) async-start(bf16[16,3,4,1024]{3,2,1,0:T(4,128)(2,1)} %select_multiply_fusion), calls=%async_computation.1 | async-start | bytes 786432 | tf_op jit(solution)/shard_map/all_to_all | solution.py:127
  40.3 0.2 select_reduce_fusion.5
  40.6 0.6 multiply_reduce_fusion
  41.2 0.6 mul.92.sub_ref
  41.8 0.6 copy.72.bias_ref
  42.4 0.4 copy.70
  42.8 1.0 reshape.290.lhs_ref.rhs_ref
  43.8 10.1 %all-to-all-done.1 = bf16[16,3,4,1024]{3,2,1,0:T(4,128)(2,1)S(1)} async-done(((bf16[16,3,4,1024]{3,2,1,0:T(4,128)(2,1)}), bf16[16,3,4,1024]{3,2,1,0:T(4,128)(2,1)S(1)}, u32[]{:S(2)}, u32[]{:S(2)}) %all-to-all-start.1) | async-done | bytes 393248 | tf_op jit(solution)/shard_map/all_to_all | solution.py:127
  53.9 0.2 multiply_reduce_fusion.1
  54.1 0.6 mul.89.sub_ref
  54.7 0.1 copy.71
  54.9 0.8 reshape.291.rhs_ref.lhs_ref
  55.7 18.3 %shard_map.77 = f32[3,1,1024]{2,1,0:T(1,128)} custom-call(s32[12]{0:T(128)} %reshape.294.valid_ref, bf16[4,64,1024]{2,1,0:T(8,128)(2,1)} %reshape.290.lhs_ref.rhs_ref, f32[4,1,1024]{2,1,0:T(1,128)} %copy.72.bias_ref, bf16[3,64,1024]{2,1,0:T(8,128)(2,1)} %reshape.291.rhs_ref.lhs_ref, f32[3,1,1024]{2,1,0:T(1,128)} %mul.89.sub_ref), custom_call_target="tpu_custom_call" | custom-call | tf_op jit(solution)/shard_map/pallas_call | solution.py:82
  74.1 0.8 broadcast_select_fusion.2
  74.9 17.0 %all_gather.4 = f32[16,3,1024]{2,1,0:T(4,128)S(1)} all-gather(f32[1,3,1024]{2,1,0:T(4,128)S(1)} %copy.73), channel_id=1, replica_groups=mesh['row'=32,'col'=16] {'col'}, dimensions={0}, use_global_device_ids=true | all-gather | bytes 208896 | tf_op jit(solution)/shard_map/all_gather | solution.py:152
  91.9 0.1 broadcast_in_dim.174
  92.0 0.1 select_reduce_fusion.3
  92.1 0.1 select_reduce_fusion.2
  92.3 0.7 fusion.5.bias_ref
  93.0 18.4 %shard_map.78 = f32[4,1,1024]{2,1,0:T(1,128)} custom-call(s32[12]{0:T(128)} %reshape.296.valid_ref, bf16[3,64,1024]{2,1,0:T(8,128)(2,1)} %reshape.291.rhs_ref.lhs_ref, f32[3,1,1024]{2,1,0:T(1,128)} %fusion.5.bias_ref, bf16[4,64,1024]{2,1,0:T(8,128)(2,1)} %reshape.290.lhs_ref.rhs_ref, f32[4,1,1024]{2,1,0:T(1,128)} %mul.92.sub_ref), custom_call_target="tpu_custom_call" | custom-call | tf_op jit(solution)/shard_map/pallas_call | solution.py:82
  111.4 0.7 copy.84
  112.1 0.9 broadcast_in_dim.180
  113.0 10.7 %all-to-all-start.2 = ((f32[32,4,1024]{2,1,0:T(4,128)}), f32[32,4,1024]{2,1,0:T(4,128)S(1)}, u32[]{:S(2)}, u32[]{:S(2)}) async-start(f32[32,4,1024]{2,1,0:T(4,128)} %broadcast_in_dim.180), calls=%async_computation.2 | async-start | bytes 1048576 | tf_op jit(solution)/shard_map/all_to_all | solution.py:174
  123.7 0.1 copy.74
  123.9 0.7 select_reduce_fusion.1
  124.5 0.8 select_reduce_fusion
  125.4 0.7 subtract_multiply_fusion
  126.1 14.3 %all-to-all-done.2 = f32[32,4,1024]{2,1,0:T(4,128)S(1)} async-done(((f32[32,4,1024]{2,1,0:T(4,128)}), f32[32,4,1024]{2,1,0:T(4,128)S(1)}, u32[]{:S(2)}, u32[]{:S(2)}) %all-to-all-start.2) | async-done | bytes 524320 | tf_op jit(solution)/shard_map/all_to_all | solution.py:174
  140.5 0.2 exponential_reduce_fusion
  140.7 0.6 subtract_multiply_fusion.1
  (38 shorter events, 1.2 us)
Async XLA Ops:
  0.6 21.2 %copy-start = (bf16[16,4,1024]{2,1,0:T(4,128)(2,1)S(1)}, bf16[16,4,1024]{2,1,0:T(4,128)(2,1)}, u32[]{:S(2)}) copy-start(bf16[16,4,1024]{2,1,0:T(4,128)(2,1)} %param.6) | copy-start | bytes 393220
  2.7 13.6 %copy-start.2 = (s32[16,8]{0,1:T(8,128)S(1)}, s32[16,8]{0,1:T(8,128)}, u32[]{:S(2)}) copy-start(s32[16,8]{0,1:T(8,128)} %param.8) | copy-start | bytes 1540
  2.7 18.5 %copy-start.1 = (f32[16,1024]{1,0:T(8,128)S(1)}, f32[16,1024]{1,0:T(8,128)}, u32[]{:S(2)}) copy-start(f32[16,1024]{1,0:T(8,128)} %param.9) | copy-start | bytes 196612
  2.7 30.4 %all-to-all-start = ((bf16[32,4,2,1024]{3,2,1,0:T(2,128)(2,1)}), bf16[32,4,2,1024]{3,2,1,0:T(2,128)(2,1)S(1)}, u32[]{:S(2)}, u32[]{:S(2)}) async-start(bf16[32,4,2,1024]{3,2,1,0:T(2,128)(2,1)} %broadcast_in_dim.157), calls=%async_computation | async-start | bytes 1048576 | tf_op jit(solution)/shard_map/all_to_all | solution.py:108
  23.7 17.4 %copy-start.3 = (f32[4,1024]{1,0:T(4,128)S(1)}, f32[4,1024]{1,0:T(4,128)}, u32[]{:S(2)}) copy-start(f32[4,1024]{1,0:T(4,128)} %param.11) | copy-start | bytes 49156
  33.0 20.8 %all-to-all-start.1 = ((bf16[16,3,4,1024]{3,2,1,0:T(4,128)(2,1)}), bf16[16,3,4,1024]{3,2,1,0:T(4,128)(2,1)S(1)}, u32[]{:S(2)}, u32[]{:S(2)}) async-start(bf16[16,3,4,1024]{3,2,1,0:T(4,128)(2,1)} %select_multiply_fusion), calls=%async_computation.1 | async-start | bytes 786432 | tf_op jit(solution)/shard_map/all_to_all | solution.py:127
  113.0 27.4 %all-to-all-start.2 = ((f32[32,4,1024]{2,1,0:T(4,128)}), f32[32,4,1024]{2,1,0:T(4,128)S(1)}, u32[]{:S(2)}, u32[]{:S(2)}) async-start(f32[32,4,1024]{2,1,0:T(4,128)} %broadcast_in_dim.180), calls=%async_computation.2 | async-start | bytes 1048576 | tf_op jit(solution)/shard_map/all_to_all | solution.py:174
  126.1 14.6 %copy-start.4 = (f32[4,1024]{1,0:T(4,128)S(1)}, f32[4,1024]{1,0:T(4,128)}, u32[]{:S(2)}) copy-start(f32[4,1024]{1,0:T(4,128)} %param.10) | copy-start | bytes 49156

commit v6 on v4

--- a/solution.py
+++ b/solution.py
@@ -157,7 +157,13 @@
     )
     src_new = blur_scale * (log_src_mass - whole)
 
-    my_pot = jnp.take(src_new, my_table, axis=0)
+    my_owner = jnp.take(owner, my_table, axis=0).reshape(SLOTS, n_col * SLOTS)
+    my_whole = masked_lse(
+        jnp.broadcast_to(row_all.reshape(1, n_col * SLOTS, pts), (SLOTS, n_col * SLOTS, pts)),
+        my_owner[:, :, None],
+        axis=1,
+    )
+    my_pot = blur_scale * (jnp.take(log_src_mass, my_table, axis=0) - my_whole)
     src_bias = (2.0 * my_pot - 2.0 * src_sq)[:, :, None]
     col_local = tile_lse(
         valid_int.T.reshape(-1), src_four, src_bias, dst_full, (2.0 * dst_sq)[:, None, :]

time: 139 us -> 142 us (1.022)
  blocking collectives: 38.8 us -> 17.5 us
  waiting for transfers between devices: 18.7 us -> 30.3 us
  starting transfers between devices: 20.6 us -> 28.6 us
  other arithmetic: 8.24 us -> 14 us
  Pallas kernels: 36.2 us -> 31.8 us
  local copies, waits for them, and re-layouts: 14.5 us -> 18 us
    all_to_all x1 -> x0, blocking collectives: 22.4 us -> none  [body(): col_all = lax.all_to_all(col_copies, 'row', 0, 0, tiled=True)]
    all_to_all x0 -> x1, waiting for transfers between devices: none -> 14.6 us  [body(): col_all = lax.all_to_all(col_copies, 'row', 0, 0, tiled=True)]
    all_to_all x0 -> x1, starting transfers between devices: none -> 8.02 us  [body(): col_all = lax.all_to_all(col_copies, 'row', 0, 0, tiled=True)]
    pallas_call x2, Pallas kernels: 36.2 us -> 31.8 us  [tile_lse(): pl.pallas_call(tile_kernel, grid_spec=grid_spec, out_shape=jax.ShapeDtype...]
    all_to_all x1, waiting for transfers between devices: 11.1 us -> 8.2 us  [body(): dst_recv = lax.all_to_all(dst_copies, 'row', 0, 0, tiled=True)]
    add x0 -> x1, local copies, waits for them, and re-layouts: none -> 1.67 us  [masked_lse(): high + jnp.log(total)]
    reduce_or x1 -> x2, other arithmetic: 0.12 us -> 1.71 us  [masked_lse(): jnp.any(mask, axis=axis)]
    sub x1, other arithmetic: 1.4 us -> 2.87 us  [body(): src_bias = (2.0 * my_pot - 2.0 * src_sq)[:, :, None]]
  transfers between devices with their start and end apart: 2 -> 3, of which waited for: 2 -> 3; matrix products, arithmetic and copies ran while one was open for 8% -> 12% of each run, Pallas kernels for 0% -> 0%
where the time goes in v6:
time: 142 us; the launch traced here: 141 us
  Pallas kernels  31.8 us (22%)
  waiting for transfers between devices  30.3 us (21%)
  starting transfers between devices  28.6 us (20%)
  local copies, waits for them, and re-layouts  18 us (13%)
  blocking collectives  17.5 us (12%)
  other arithmetic  14 us (10%)
    pallas_call x2, Pallas kernels, tile_lse(): pl.pallas_call(tile_kernel, grid_spec=grid_spec, out_shape=jax.ShapeDtype...  31.8 us
    all_gather x1, blocking collectives, body(): row_all = lax.all_gather(row_local, 'col', axis=0, tiled=False)  17.5 us
    all_to_all x1, waiting for transfers between devices, body(): col_all = lax.all_to_all(col_copies, 'row', 0, 0, tiled=True)  14.6 us
    all_to_all x1, starting transfers between devices, body(): dst_recv = lax.all_to_all(dst_copies, 'row', 0, 0, tiled=True)  13.4 us
    all_to_all x1, waiting for transfers between devices, body(): dst_recv = lax.all_to_all(dst_copies, 'row', 0, 0, tiled=True)  8.2 us
    all_to_all x1, starting transfers between devices, body(): col_all = lax.all_to_all(col_copies, 'row', 0, 0, tiled=True)  8.02 us
    all_to_all x1, waiting for transfers between devices, body(): recv = lax.all_to_all(send, 'col', 0, 0, tiled=True)  7.57 us
    all_to_all x1, starting transfers between devices, body(): recv = lax.all_to_all(send, 'col', 0, 0, tiled=True)  7.21 us
  transfers between devices with their start and end apart: 3, of which 3 were waited for; matrix products, arithmetic and copies ran while one was open for 12% of the time, Pallas kernels for 0%

profile of v6, /device:TPU:6, one launch (start us, length us, event | category | flops | bytes accessed | tf_op | source)
XLA Modules:
  0.0 141.2 jit_solution(13754220300084064875)
XLA Ops:
  0.7 2.0 %broadcast_in_dim.157 = bf16[32,4,2,1024]{3,2,1,0:T(2,128)(2,1)} broadcast(bf16[4,2,1024]{2,1,0:T(2,128)(2,1)} %param.7), dimensions={1,2,3} | broadcast | bytes 540672 | tf_op jit(solution)/shard_map/broadcast_in_dim | solution.py:106
  2.7 13.4 %all-to-all-start = ((bf16[32,4,2,1024]{3,2,1,0:T(2,128)(2,1)}), bf16[32,4,2,1024]{3,2,1,0:T(2,128)(2,1)S(1)}, u32[]{:S(2)}, u32[]{:S(2)}) async-start(bf16[32,4,2,1024]{3,2,1,0:T(2,128)(2,1)} %broadcast_in_dim.157), calls=%async_computation | async-start | bytes 1048576 | tf_op jit(solution)/shard_map/all_to_all | solution.py:107
  16.6 0.2 fusion.3
  16.8 0.2 select_reduce_fusion.4
  16.9 0.2 dynamic-slice_reduce_fusion
  17.2 0.2 dynamic-slice_reduce_fusion.1
  17.4 0.6 gather_fusion
  18.1 0.2 compare_reduce_fusion
  18.3 0.7 reshape.307.valid_ref
  19.3 0.7 reshape.309.valid_ref
  20.0 0.9 fusion.11
  20.9 0.6 gather_fusion.3
  21.7 0.6 gather_fusion.2
  22.3 0.5 copy.89
  22.8 0.9 gather_fusion.1
  23.7 1.0 select_multiply_fusion
  24.7 8.2 %all-to-all-done = bf16[32,4,2,1024]{3,2,1,0:T(2,128)(2,1)S(1)} async-done(((bf16[32,4,2,1024]{3,2,1,0:T(2,128)(2,1)}), bf16[32,4,2,1024]{3,2,1,0:T(2,128)(2,1)S(1)}, u32[]{:S(2)}, u32[]{:S(2)}) %all-to-all-start) | async-done | bytes 524320 | tf_op jit(solution)/shard_map/all_to_all | solution.py:107
  32.9 7.2 %all-to-all-start.1 = ((bf16[16,3,4,1024]{3,2,1,0:T(4,128)(2,1)}), bf16[16,3,4,1024]{3,2,1,0:T(4,128)(2,1)S(1)}, u32[]{:S(2)}, u32[]{:S(2)}) async-start(bf16[16,3,4,1024]{3,2,1,0:T(4,128)(2,1)} %select_multiply_fusion), calls=%async_computation.1 | async-start | bytes 786432 | tf_op jit(solution)/shard_map/all_to_all | solution.py:126
  40.2 0.8 select_reduce_fusion.5
  41.0 0.7 broadcast_select_fusion.2
  41.6 0.4 copy.83
  42.0 1.0 reshape.303.lhs_ref.rhs_ref
  43.0 0.6 multiply_reduce_fusion
  43.6 2.0 %copy.85.bias_ref = f32[4,1024,1]{2,1,0:T(8,128)} copy(f32[4,1024,1]{1,0,2:T(4,128)S(1)} %get-tuple-element.9) | data formatting | bytes 32768 | tf_op jit(solution)/shard_map/broadcast_in_dim | solution.py:145
  45.6 0.6 mul.99.sub_ref
  46.2 7.6 %all-to-all-done.1 = bf16[16,3,4,1024]{3,2,1,0:T(4,128)(2,1)S(1)} async-done(((bf16[16,3,4,1024]{3,2,1,0:T(4,128)(2,1)}), bf16[16,3,4,1024]{3,2,1,0:T(4,128)(2,1)S(1)}, u32[]{:S(2)}, u32[]{:S(2)}) %all-to-all-start.1) | async-done | bytes 393248 | tf_op jit(solution)/shard_map/all_to_all | solution.py:126
  53.9 0.8 reshape.304.rhs_ref.lhs_ref
  54.8 0.2 multiply_reduce_fusion.1
  55.0 0.6 mul.95.sub_ref
  55.6 15.9 %shard_map.77 = f32[3,1,1024]{2,1,0:T(1,128)} custom-call(s32[12]{0:T(128)} %reshape.307.valid_ref, bf16[4,64,1024]{2,1,0:T(8,128)(2,1)} %reshape.303.lhs_ref.rhs_ref, f32[4,1024,1]{2,1,0:T(8,128)} %copy.85.bias_ref, bf16[3,64,1024]{2,1,0:T(8,128)(2,1)} %reshape.304.rhs_ref.lhs_ref, f32[3,1,1024]{2,1,0:T(1,128)} %mul.95.sub_ref), custom_call_target="tpu_custom_call" | custom-call | tf_op jit(solution)/shard_map/pallas_call | solution.py:81
  71.5 0.8 broadcast_select_fusion
  72.3 17.5 %all_gather.4 = f32[16,3,1024]{2,1,0:T(4,128)S(1)} all-gather(f32[1,3,1024]{2,1,0:T(4,128)S(1)} %copy.86), channel_id=1, replica_groups=mesh['row'=32,'col'=16] {'col'}, dimensions={0}, use_global_device_ids=true | all-gather | bytes 208896 | tf_op jit(solution)/shard_map/all_gather | solution.py:151
  89.8 0.5 copy.92
  90.3 0.8 broadcast_in_dim.174
  91.0 1.1 select_reduce_fusion.3
  92.1 1.1 select_reduce_fusion.2
  93.2 1.7 %copy.91 = f32[3,1024,1]{2,1,0:T(8,128)} copy(f32[3,1024,1]{1,0,2:T(4,128)S(1)} %add_bitcast_fusion) | data formatting | bytes 24576 | tf_op jit(solution)/shard_map/add | solution.py:93
  94.9 2.9 %subtract_subtract_fusion.bias_ref = f32[3,1024,1]{2,1,0:T(8,128)} fusion(f32[3,1024,1]{2,1,0:T(8,128)S(1)} %copy.92, f32[3,1024,1]{2,1,0:T(8,128)} %copy.91, f32[3,1024,1]{2,1,0:T(8,128)S(1)} %copy.89, pred[3]{0:T(512)(128)(4,1)} %select_reduce_fusion.5, pred[3]{0:T(512)(128)(4,1)} %copy-done.8), kind=kLoop, calls=%fused_computation.6 | loop fusion | flops 12288 | bytes 49158 | tf_op jit(solution)/shard_map/sub | solution.py:167
  97.8 15.9 %shard_map.78 = f32[4,1,1024]{2,1,0:T(1,128)} custom-call(s32[12]{0:T(128)} %reshape.309.valid_ref, bf16[3,64,1024]{2,1,0:T(8,128)(2,1)} %reshape.304.rhs_ref.lhs_ref, f32[3,1024,1]{2,1,0:T(8,128)} %subtract_subtract_fusion.bias_ref, bf16[4,64,1024]{2,1,0:T(8,128)(2,1)} %reshape.303.lhs_ref.rhs_ref, f32[4,1,1024]{2,1,0:T(1,128)} %mul.99.sub_ref), custom_call_target="tpu_custom_call" | custom-call | tf_op jit(solution)/shard_map/pallas_call | solution.py:81
  113.7 0.7 copy.100
  114.4 0.9 broadcast_in_dim.180
  115.3 8.0 %all-to-all-start.2 = ((f32[32,4,1024]{2,1,0:T(4,128)}), f32[32,4,1024]{2,1,0:T(4,128)S(1)}, u32[]{:S(2)}, u32[]{:S(2)}) async-start(f32[32,4,1024]{2,1,0:T(4,128)} %broadcast_in_dim.180), calls=%async_computation.2 | async-start | bytes 1048576 | tf_op jit(solution)/shard_map/all_to_all | solution.py:173
  123.5 0.7 select_reduce_fusion.1
  124.2 0.8 select_reduce_fusion
  125.0 0.7 subtract_multiply_fusion
  125.7 14.6 %all-to-all-done.2 = f32[32,4,1024]{2,1,0:T(4,128)S(1)} async-done(((f32[32,4,1024]{2,1,0:T(4,128)}), f32[32,4,1024]{2,1,0:T(4,128)S(1)}, u32[]{:S(2)}, u32[]{:S(2)}) %all-to-all-start.2) | async-done | bytes 524320 | tf_op jit(solution)/shard_map/all_to_all | solution.py:173
  140.4 0.2 exponential_reduce_fusion
  140.6 0.6 subtract_multiply_fusion.1
  (51 shorter events, 1.7 us)
Async XLA Ops:
  0.6 22.2 %copy-start = (bf16[16,4,1024]{2,1,0:T(4,128)(2,1)S(1)}, bf16[16,4,1024]{2,1,0:T(4,128)(2,1)}, u32[]{:S(2)}) copy-start(bf16[16,4,1024]{2,1,0:T(4,128)(2,1)} %param.6) | copy-start | bytes 393220
  0.6 15.5 %copy-start.5 = (s32[16,8]{0,1:T(8,128)S(1)}, s32[16,8]{0,1:T(8,128)}, u32[]{:S(2)}) copy-start(s32[16,8]{0,1:T(8,128)} %param.8) | copy-start | bytes 1540
  0.7 21.0 %copy-start.1 = (f32[16,1024]{1,0:T(8,128)S(1)}, f32[16,1024]{1,0:T(8,128)}, u32[]{:S(2)}) copy-start(f32[16,1024]{1,0:T(8,128)} %param.9) | copy-start | bytes 196612
  2.7 30.2 %all-to-all-start = ((bf16[32,4,2,1024]{3,2,1,0:T(2,128)(2,1)}), bf16[32,4,2,1024]{3,2,1,0:T(2,128)(2,1)S(1)}, u32[]{:S(2)}, u32[]{:S(2)}) async-start(bf16[32,4,2,1024]{3,2,1,0:T(2,128)(2,1)} %broadcast_in_dim.157), calls=%async_computation | async-start | bytes 1048576 | tf_op jit(solution)/shard_map/all_to_all | solution.py:107
  17.1 23.9 %copy-start.8 = (pred[3]{0:T(512)(128)(4,1)}, pred[3]{0:T(512)(128)(4,1)S(1)}, u32[]{:S(2)}) copy-start(pred[3]{0:T(512)(128)(4,1)S(1)} %compare_and_fusion.1) | copy-start | bytes 13
  20.9 1.4 copy-start.3
  24.7 18.8 %copy-start.6 = (f32[4,1024]{1,0:T(4,128)S(1)}, f32[4,1024]{1,0:T(4,128)}, u32[]{:S(2)}) copy-start(f32[4,1024]{1,0:T(4,128)} %param.11) | copy-start | bytes 49156
  32.9 20.8 %all-to-all-start.1 = ((bf16[16,3,4,1024]{3,2,1,0:T(4,128)(2,1)}), bf16[16,3,4,1024]{3,2,1,0:T(4,128)(2,1)S(1)}, u32[]{:S(2)}, u32[]{:S(2)}) async-start(bf16[16,3,4,1024]{3,2,1,0:T(4,128)(2,1)} %select_multiply_fusion), calls=%async_computation.1 | async-start | bytes 786432 | tf_op jit(solution)/shard_map/all_to_all | solution.py:126
  113.7 9.8 %copy-start.4 = (pred[16,16,3]{1,2,0:T(4,128)(4,1)S(1)}, pred[16,16,3]{1,2,0:T(4,128)(4,1)}, u32[]{:S(2)}) copy-start(pred[16,16,3]{1,2,0:T(4,128)(4,1)} %copy-done.3) | copy-start | bytes 2308
  115.3 9.7 %copy-start.2 = (f32[16,1024]{1,0:T(8,128)S(1)}, f32[16,1024]{1,0:T(8,128)}, u32[]{:S(2)}) copy-start(f32[16,1024]{1,0:T(8,128)} %param.9) | copy-start | bytes 196612
  115.3 9.7 %copy-start.9 = (pred[16]{0:T(512)(128)(4,1)S(1)}, pred[16]{0:T(512)(128)(4,1)}, u32[]{:S(2)}) copy-start(pred[16]{0:T(512)(128)(4,1)} %get-tuple-element.6) | copy-start | bytes 52
  115.3 25.0 %all-to-all-start.2 = ((f32[32,4,1024]{2,1,0:T(4,128)}), f32[32,4,1024]{2,1,0:T(4,128)S(1)}, u32[]{:S(2)}, u32[]{:S(2)}) async-start(f32[32,4,1024]{2,1,0:T(4,128)} %broadcast_in_dim.180), calls=%async_computation.2 | async-start | bytes 1048576 | tf_op jit(solution)/shard_map/all_to_all | solution.py:173
  123.5 17.1 %copy-start.7 = (f32[4,1024]{1,0:T(4,128)S(1)}, f32[4,1024]{1,0:T(4,128)}, u32[]{:S(2)}) copy-start(f32[4,1024]{1,0:T(4,128)} %param.10) | copy-start | bytes 49156

commit v7 on v6

--- a/solution.py
+++ b/solution.py
@@ -165,6 +165,7 @@
     )
     my_pot = blur_scale * (jnp.take(log_src_mass, my_table, axis=0) - my_whole)
     src_bias = (2.0 * my_pot - 2.0 * src_sq)[:, :, None]
+    src_new, src_bias = lax.optimization_barrier((src_new, src_bias))
     col_local = tile_lse(
         valid_int.T.reshape(-1), src_four, src_bias, dst_full, (2.0 * dst_sq)[:, None, :]
     )[:, 0, :]

time: 142 us -> 143 us (level)
  blocking collectives: 17.5 us -> 36.2 us
  waiting for transfers between devices: 30.3 us -> 15.8 us
  starting transfers between devices: 28.6 us -> 20.6 us
  Pallas kernels: 31.8 us -> 37.3 us
  local copies, waits for them, and re-layouts: 18 us -> 16.5 us
    all_to_all x0 -> x1, blocking collectives: none -> 21.3 us  [body(): col_all = lax.all_to_all(col_copies, 'row', 0, 0, tiled=True)]
    all_to_all x1 -> x0, waiting for transfers between devices: 14.6 us -> none  [body(): col_all = lax.all_to_all(col_copies, 'row', 0, 0, tiled=True)]
    all_to_all x1 -> x0, starting transfers between devices: 8.02 us -> none  [body(): col_all = lax.all_to_all(col_copies, 'row', 0, 0, tiled=True)]
    pallas_call x2, Pallas kernels: 31.8 us -> 37.3 us  [tile_lse(): pl.pallas_call(tile_kernel, grid_spec=grid_spec, out_shape=jax.ShapeDtype...]
    all_gather x1, blocking collectives: 17.5 us -> 14.9 us  [body(): row_all = lax.all_gather(row_local, 'col', axis=0, tiled=False)]
  transfers between devices with their start and end apart: 3 -> 2, of which waited for: 3 -> 2; matrix products, arithmetic and copies ran while one was open for 12% -> 10% of each run, Pallas kernels for 0% -> 0%
where the time goes in v7:
time: 143 us; the launch traced here: 142 us
  Pallas kernels  37.3 us (26%)
  blocking collectives  36.2 us (25%)
  starting transfers between devices  20.6 us (14%)
  local copies, waits for them, and re-layouts  16.5 us (12%)
  waiting for transfers between devices  15.8 us (11%)
  other arithmetic  14.2 us (10%)
    pallas_call x2, Pallas kernels, tile_lse(): pl.pallas_call(tile_kernel, grid_spec=grid_spec, out_shape=jax.ShapeDtype...  37.3 us
    all_to_all x1, blocking collectives, body(): col_all = lax.all_to_all(col_copies, 'row', 0, 0, tiled=True)  21.3 us
    all_gather x1, blocking collectives, body(): row_all = lax.all_gather(row_local, 'col', axis=0, tiled=False)  14.9 us
    all_to_all x1, starting transfers between devices, body(): dst_recv = lax.all_to_all(dst_copies, 'row', 0, 0, tiled=True)  13.4 us
    all_to_all x1, waiting for transfers between devices, body(): dst_recv = lax.all_to_all(dst_copies, 'row', 0, 0, tiled=True)  8.21 us
    all_to_all x1, waiting for transfers between devices, body(): recv = lax.all_to_all(send, 'col', 0, 0, tiled=True)  7.63 us
    all_to_all x1, starting transfers between devices, body(): recv = lax.all_to_all(send, 'col', 0, 0, tiled=True)  7.21 us
    sub x1, other arithmetic, body(): src_bias = (2.0 * my_pot - 2.0 * src_sq)[:, :, None]  2.87 us
  transfers between devices with their start and end apart: 2, of which 2 were waited for; matrix products, arithmetic and copies ran while one was open for 10% of the time, Pallas kernels for 0%

profile of v7, /device:TPU:6, one launch (start us, length us, event | category | flops | bytes accessed | tf_op | source)
XLA Modules:
  0.0 141.5 jit_solution(1476024361335592360)
XLA Ops:
  0.7 2.0 %broadcast_in_dim.157 = bf16[32,4,2,1024]{3,2,1,0:T(2,128)(2,1)} broadcast(bf16[4,2,1024]{2,1,0:T(2,128)(2,1)} %param.7), dimensions={1,2,3} | broadcast | bytes 540672 | tf_op jit(solution)/shard_map/broadcast_in_dim | solution.py:106
  2.7 13.4 %all-to-all-start = ((bf16[32,4,2,1024]{3,2,1,0:T(2,128)(2,1)}), bf16[32,4,2,1024]{3,2,1,0:T(2,128)(2,1)S(1)}, u32[]{:S(2)}, u32[]{:S(2)}) async-start(bf16[32,4,2,1024]{3,2,1,0:T(2,128)(2,1)} %broadcast_in_dim.157), calls=%async_computation | async-start | bytes 1048576 | tf_op jit(solution)/shard_map/all_to_all | solution.py:107
  16.6 0.2 fusion.3
  16.7 0.2 select_reduce_fusion.4
  16.9 0.2 dynamic-slice_reduce_fusion
  17.2 0.2 dynamic-slice_reduce_fusion.1
  17.4 0.6 gather_fusion
  18.1 0.2 compare_reduce_fusion
  18.3 0.7 reshape.307.valid_ref
  19.2 1.0 fusion.11
  20.2 0.6 gather_fusion.3
  20.8 0.1 copy.89
  21.0 0.6 gather_fusion.2
  21.6 0.5 copy.88
  22.2 0.6 reshape.309.valid_ref
  22.8 0.9 gather_fusion.1
  23.7 1.0 select_multiply_fusion
  24.7 8.2 %all-to-all-done = bf16[32,4,2,1024]{3,2,1,0:T(2,128)(2,1)S(1)} async-done(((bf16[32,4,2,1024]{3,2,1,0:T(2,128)(2,1)}), bf16[32,4,2,1024]{3,2,1,0:T(2,128)(2,1)S(1)}, u32[]{:S(2)}, u32[]{:S(2)}) %all-to-all-start) | async-done | bytes 524320 | tf_op jit(solution)/shard_map/all_to_all | solution.py:107
  32.9 7.2 %all-to-all-start.1 = ((bf16[16,3,4,1024]{3,2,1,0:T(4,128)(2,1)}), bf16[16,3,4,1024]{3,2,1,0:T(4,128)(2,1)S(1)}, u32[]{:S(2)}, u32[]{:S(2)}) async-start(bf16[16,3,4,1024]{3,2,1,0:T(4,128)(2,1)} %select_multiply_fusion), calls=%async_computation.1 | async-start | bytes 786432 | tf_op jit(solution)/shard_map/all_to_all | solution.py:126
  40.2 0.8 select_reduce_fusion.5
  40.9 0.7 broadcast_select_fusion.2
  41.6 0.4 copy.83
  41.9 1.0 reshape.303.lhs_ref.rhs_ref
  42.9 0.6 multiply_reduce_fusion
  43.5 2.0 %copy.85.bias_ref = f32[4,1024,1]{2,1,0:T(8,128)} copy(f32[4,1024,1]{1,0,2:T(4,128)S(1)} %get-tuple-element.13) | data formatting | bytes 32768 | tf_op jit(solution)/shard_map/broadcast_in_dim | solution.py:145
  45.5 0.6 mul.99.sub_ref
  46.2 7.6 %all-to-all-done.1 = bf16[16,3,4,1024]{3,2,1,0:T(4,128)(2,1)S(1)} async-done(((bf16[16,3,4,1024]{3,2,1,0:T(4,128)(2,1)}), bf16[16,3,4,1024]{3,2,1,0:T(4,128)(2,1)S(1)}, u32[]{:S(2)}, u32[]{:S(2)}) %all-to-all-start.1) | async-done | bytes 393248 | tf_op jit(solution)/shard_map/all_to_all | solution.py:126
  53.8 0.1 copy.84
  53.9 0.8 reshape.304.rhs_ref.lhs_ref
  54.8 0.2 multiply_reduce_fusion.1
  55.0 0.6 mul.95.sub_ref
  55.6 18.6 %shard_map.77 = f32[3,1,1024]{2,1,0:T(1,128)} custom-call(s32[12]{0:T(128)} %reshape.307.valid_ref, bf16[4,64,1024]{2,1,0:T(8,128)(2,1)} %reshape.303.lhs_ref.rhs_ref, f32[4,1024,1]{2,1,0:T(8,128)} %copy.85.bias_ref, bf16[3,64,1024]{2,1,0:T(8,128)(2,1)} %reshape.304.rhs_ref.lhs_ref, f32[3,1,1024]{2,1,0:T(1,128)} %mul.95.sub_ref), custom_call_target="tpu_custom_call" | custom-call | tf_op jit(solution)/shard_map/pallas_call | solution.py:81
  74.3 0.8 broadcast_select_fusion
  75.1 14.9 %all_gather.4 = f32[16,3,1024]{2,1,0:T(4,128)S(1)} all-gather(f32[1,3,1024]{2,1,0:T(4,128)S(1)} %copy.86), channel_id=1, replica_groups=mesh['row'=32,'col'=16] {'col'}, dimensions={0}, use_global_device_ids=true | all-gather | bytes 208896 | tf_op jit(solution)/shard_map/all_gather | solution.py:151
  89.9 0.1 copy.87
  90.2 0.7 select_reduce_fusion.1
  90.9 1.4 %select_reduce_fusion = f32[16,1024]{1,0:T(8,128)} fusion(f32[16,1024]{1,0:T(8,128)S(1)} %select_reduce_fusion.1, f32[16,3,1024]{2,0,1:T(8,128)S(1)} %copy.87, pred[16,16,3]{1,2,0:T(4,128)(4,1)S(1)} %get-tuple-element.11), kind=kLoop, calls=%fused_computation.4 | loop fusion | flops 2342912 | bytes 328448 | tf_op jit(solution)/shard_map/reduce_sum | solution.py:90
  92.3 0.5 copy.91
  92.8 0.8 select_reduce_fusion.3
  93.6 0.8 select_reduce_fusion.2
  94.5 1.7 %copy.90 = f32[3,1024,1]{2,1,0:T(8,128)} copy(f32[3,1024,1]{1,0,2:T(4,128)S(1)} %add_bitcast_fusion) | data formatting | bytes 24576 | tf_op jit(solution)/shard_map/add | solution.py:93
  96.2 0.7 subtract_multiply_fusion
  96.9 2.9 %subtract_subtract_fusion.bias_ref = f32[3,1024,1]{2,1,0:T(8,128)} fusion(f32[3,1024,1]{2,1,0:T(8,128)S(1)} %copy.91, f32[3,1024,1]{2,1,0:T(8,128)} %copy.90, f32[3,1024,1]{2,1,0:T(8,128)S(1)} %copy.88, pred[3]{0:T(512)(128)(4,1)S(1)} %copy-done.11, pred[3]{0:T(512)(128)(4,1)S(1)} %copy-done.9), kind=kLoop, calls=%fused_computation.6 | loop fusion | flops 12288 | bytes 49158 | tf_op jit(solution)/shard_map/sub | solution.py:167
  99.8 18.7 %shard_map.78 = f32[4,1,1024]{2,1,0:T(1,128)} custom-call(s32[12]{0:T(128)} %reshape.309.valid_ref, bf16[3,64,1024]{2,1,0:T(8,128)(2,1)} %reshape.304.rhs_ref.lhs_ref, f32[3,1024,1]{2,1,0:T(8,128)} %subtract_subtract_fusion.bias_ref, bf16[4,64,1024]{2,1,0:T(8,128)(2,1)} %reshape.303.lhs_ref.rhs_ref, f32[4,1,1024]{2,1,0:T(1,128)} %mul.99.sub_ref), custom_call_target="tpu_custom_call" | custom-call | tf_op jit(solution)/shard_map/pallas_call | solution.py:81
  118.4 0.7 copy.100
  119.3 21.3 %all_to_all.15 = f32[32,4,1024]{2,1,0:T(4,128)S(1)} all-to-all(f32[32,4,1024]{2,1,0:T(4,128)S(1)} %broadcast_in_dim.180), channel_id=1, replica_groups=mesh['row'=32,'col'=16] {'row'}, dimensions={0} | all-to-all | bytes 1048576 | tf_op jit(solution)/shard_map/all_to_all | solution.py:174
  140.7 0.2 exponential_reduce_fusion
  140.9 0.6 subtract_multiply_fusion.1
  (54 shorter events, 1.5 us)
Async XLA Ops:
  0.6 22.2 %copy-start = (bf16[16,4,1024]{2,1,0:T(4,128)(2,1)S(1)}, bf16[16,4,1024]{2,1,0:T(4,128)(2,1)}, u32[]{:S(2)}) copy-start(bf16[16,4,1024]{2,1,0:T(4,128)(2,1)} %param.6) | copy-start | bytes 393220
  0.6 15.5 %copy-start.5 = (s32[16,8]{0,1:T(8,128)S(1)}, s32[16,8]{0,1:T(8,128)}, u32[]{:S(2)}) copy-start(s32[16,8]{0,1:T(8,128)} %param.8) | copy-start | bytes 1540
  0.7 20.3 %copy-start.1 = (f32[16,1024]{1,0:T(8,128)S(1)}, f32[16,1024]{1,0:T(8,128)}, u32[]{:S(2)}) copy-start(f32[16,1024]{1,0:T(8,128)} %param.9) | copy-start | bytes 196612
  2.7 30.2 %all-to-all-start = ((bf16[32,4,2,1024]{3,2,1,0:T(2,128)(2,1)}), bf16[32,4,2,1024]{3,2,1,0:T(2,128)(2,1)S(1)}, u32[]{:S(2)}, u32[]{:S(2)}) async-start(bf16[32,4,2,1024]{3,2,1,0:T(2,128)(2,1)} %broadcast_in_dim.157), calls=%async_computation | async-start | bytes 1048576 | tf_op jit(solution)/shard_map/all_to_all | solution.py:107
  17.1 23.8 %copy-start.8 = (pred[3]{0:T(512)(128)(4,1)}, pred[3]{0:T(512)(128)(4,1)S(1)}, u32[]{:S(2)}) copy-start(pred[3]{0:T(512)(128)(4,1)S(1)} %compare_and_fusion.1) | copy-start | bytes 13
  24.7 18.8 %copy-start.6 = (f32[4,1024]{1,0:T(4,128)S(1)}, f32[4,1024]{1,0:T(4,128)}, u32[]{:S(2)}) copy-start(f32[4,1024]{1,0:T(4,128)} %param.11) | copy-start | bytes 49156
  32.9 20.8 %all-to-all-start.1 = ((bf16[16,3,4,1024]{3,2,1,0:T(4,128)(2,1)}), bf16[16,3,4,1024]{3,2,1,0:T(4,128)(2,1)S(1)}, u32[]{:S(2)}, u32[]{:S(2)}) async-start(bf16[16,3,4,1024]{3,2,1,0:T(4,128)(2,1)} %select_multiply_fusion), calls=%async_computation.1 | async-start | bytes 786432 | tf_op jit(solution)/shard_map/all_to_all | solution.py:126
  90.8 1.4 %copy-start.2 = (f32[16,1024]{1,0:T(8,128)}, f32[16,1024]{1,0:T(8,128)S(1)}, u32[]{:S(2)}) copy-start(f32[16,1024]{1,0:T(8,128)S(1)} %select_reduce_fusion.1) | copy-start | bytes 196612
  92.8 3.4 %copy-start.10 = (pred[16]{0:T(512)(128)(4,1)S(1)}, pred[16]{0:T(512)(128)(4,1)}, u32[]{:S(2)}) copy-start(pred[16]{0:T(512)(128)(4,1)} %get-tuple-element.10) | copy-start | bytes 52
  92.8 4.1 %copy-start.9 = (pred[3]{0:T(512)(128)(4,1)S(1)}, pred[3]{0:T(512)(128)(4,1)}, u32[]{:S(2)}) copy-start(pred[3]{0:T(512)(128)(4,1)} %copy-done.8) | copy-start | bytes 13
  92.8 4.1 %copy-start.11 = (pred[3]{0:T(512)(128)(4,1)S(1)}, pred[3]{0:T(512)(128)(4,1)}, u32[]{:S(2)}) copy-start(pred[3]{0:T(512)(128)(4,1)} %select_reduce_fusion.5) | copy-start | bytes 13
  94.5 1.7 %copy-start.3 = (f32[16,1024]{1,0:T(8,128)S(1)}, f32[16,1024]{1,0:T(8,128)}, u32[]{:S(2)}) copy-start(f32[16,1024]{1,0:T(8,128)} %copy-done.2) | copy-start | bytes 196612
  94.5 1.7 %copy-start.4 = (f32[16,1024]{1,0:T(8,128)S(1)}, f32[16,1024]{1,0:T(8,128)}, u32[]{:S(2)}) copy-start(f32[16,1024]{1,0:T(8,128)} %select_reduce_fusion) | copy-start | bytes 196612
  118.4 22.4 %copy-start.7 = (f32[4,1024]{1,0:T(4,128)S(1)}, f32[4,1024]{1,0:T(4,128)}, u32[]{:S(2)}) copy-start(f32[4,1024]{1,0:T(4,128)} %param.10) | copy-start | bytes 49156

commit v8 on v4

--- a/solution.py
+++ b/solution.py
@@ -163,8 +163,7 @@
         valid_int.T.reshape(-1), src_four, src_bias, dst_full, (2.0 * dst_sq)[:, None, :]
     )[:, 0, :]
 
-    col_copies = jnp.broadcast_to(col_local[None], (n_row,) + col_local.shape)
-    col_all = lax.all_to_all(col_copies, "row", 0, 0, tiled=True)
+    col_all = lax.all_gather(col_local, "row", axis=0, tiled=False)
     col_high = jnp.max(col_all, axis=0)
     col_whole = col_high + jnp.log(jnp.sum(jnp.exp(col_all - col_high[None]), axis=0))
     dst_new = blur_scale * (log_dst_mass - col_whole)

time: 139 us -> 164 us (1.18)
  blocking collectives: 38.8 us -> 66.5 us
  Pallas kernels: 36.2 us -> 33.6 us
    all_gather x0 -> x1, blocking collectives: none -> 49.5 us  [body(): col_all = lax.all_gather(col_local, 'row', axis=0, tiled=False)]
    all_to_all x1 -> x0, blocking collectives: 22.4 us -> none  [body(): col_all = lax.all_to_all(col_copies, 'row', 0, 0, tiled=True)]
    pallas_call x2, Pallas kernels: 36.2 us -> 33.6 us  [tile_lse(): pl.pallas_call(tile_kernel, grid_spec=grid_spec, out_shape=jax.ShapeDtype...]
  transfers between devices with their start and end apart: 2 -> 2, of which waited for: 2 -> 2; matrix products, arithmetic and copies ran while one was open for 8% -> 7% of each run, Pallas kernels for 0% -> 0%
where the time goes in v8:
time: 164 us
  blocking collectives  66.5 us (41%)
  Pallas kernels  33.6 us (20%)
  starting transfers between devices  20.6 us (13%)
  waiting for transfers between devices  18.7 us (11%)
  local copies, waits for them, and re-layouts  13.8 us (8%)
  other arithmetic  9.48 us (6%)
    all_gather x1, blocking collectives, body(): col_all = lax.all_gather(col_local, 'row', axis=0, tiled=False)  49.5 us
    pallas_call x2, Pallas kernels, tile_lse(): pl.pallas_call(tile_kernel, grid_spec=grid_spec, out_shape=jax.ShapeDtype...  33.6 us
    all_gather x1, blocking collectives, body(): row_all = lax.all_gather(row_local, 'col', axis=0, tiled=False)  17.1 us
    all_to_all x1, starting transfers between devices, body(): dst_recv = lax.all_to_all(dst_copies, 'row', 0, 0, tiled=True)  13.4 us
    all_to_all x1, waiting for transfers between devices, body(): dst_recv = lax.all_to_all(dst_copies, 'row', 0, 0, tiled=True)  11.1 us
    all_to_all x1, waiting for transfers between devices, body(): recv = lax.all_to_all(send, 'col', 0, 0, tiled=True)  7.54 us
    all_to_all x1, starting transfers between devices, body(): recv = lax.all_to_all(send, 'col', 0, 0, tiled=True)  7.21 us
  transfers between devices with their start and end apart: 2, of which 2 were waited for; matrix products, arithmetic and copies ran while one was open for 7% of the time, Pallas kernels for 0%

profile of v8, /device:TPU:6, one launch (start us, length us, event | category | flops | bytes accessed | tf_op | source)
XLA Modules:
  0.0 163.6 jit_solution(8842950854329423087)
XLA Ops:
  0.6 2.0 %broadcast_in_dim.102 = bf16[32,4,2,1024]{3,2,1,0:T(2,128)(2,1)} broadcast(bf16[4,2,1024]{2,1,0:T(2,128)(2,1)} %param.7), dimensions={1,2,3} | broadcast | bytes 540672 | tf_op jit(solution)/shard_map/broadcast_in_dim | solution.py:106
  2.7 13.4 %all-to-all-start = ((bf16[32,4,2,1024]{3,2,1,0:T(2,128)(2,1)}), bf16[32,4,2,1024]{3,2,1,0:T(2,128)(2,1)S(1)}, u32[]{:S(2)}, u32[]{:S(2)}) async-start(bf16[32,4,2,1024]{3,2,1,0:T(2,128)(2,1)} %broadcast_in_dim.102), calls=%async_computation | async-start | bytes 1048576 | tf_op jit(solution)/shard_map/all_to_all | solution.py:107
  16.1 0.7 add_select_fusion
  16.8 0.8 copy.74
  17.6 0.1 fusion
  17.9 0.2 fusion.3
  18.1 0.2 select_reduce_fusion.2
  18.2 0.1 copy.76
  18.3 0.2 dynamic-slice_reduce_fusion
  18.5 0.2 dynamic-slice_reduce_fusion.1
  18.8 0.1 copy.75
  18.9 0.6 gather_fusion
  19.5 0.9 gather_fusion.1
  20.5 0.2 compare_reduce_fusion
  20.7 1.0 select_multiply_fusion
  21.8 11.1 %all-to-all-done = bf16[32,4,2,1024]{3,2,1,0:T(2,128)(2,1)S(1)} async-done(((bf16[32,4,2,1024]{3,2,1,0:T(2,128)(2,1)}), bf16[32,4,2,1024]{3,2,1,0:T(2,128)(2,1)S(1)}, u32[]{:S(2)}, u32[]{:S(2)}) %all-to-all-start) | async-done | bytes 524320 | tf_op jit(solution)/shard_map/all_to_all | solution.py:107
  32.9 7.2 %all-to-all-start.1 = ((bf16[16,3,4,1024]{3,2,1,0:T(4,128)(2,1)}), bf16[16,3,4,1024]{3,2,1,0:T(4,128)(2,1)S(1)}, u32[]{:S(2)}, u32[]{:S(2)}) async-start(bf16[16,3,4,1024]{3,2,1,0:T(4,128)(2,1)} %select_multiply_fusion), calls=%async_computation.1 | async-start | bytes 786432 | tf_op jit(solution)/shard_map/all_to_all | solution.py:126
  40.2 0.6 reshape.248.valid_ref
  40.8 0.1 fusion.11
  40.9 0.1 copy.82
  41.0 0.6 reshape.250.valid_ref
  41.6 0.4 copy.77
  42.0 1.0 reshape.244.lhs_ref.rhs_ref
  43.0 0.6 multiply_reduce_fusion
  43.6 2.0 %copy.79.bias_ref = f32[4,1024,1]{2,1,0:T(8,128)} copy(f32[4,1024,1]{1,0,2:T(4,128)S(1)} %get-tuple-element.9) | data formatting | bytes 32768 | tf_op jit(solution)/shard_map/broadcast_in_dim | solution.py:145
  45.6 0.6 mul.106.sub_ref
  46.2 7.5 %all-to-all-done.1 = bf16[16,3,4,1024]{3,2,1,0:T(4,128)(2,1)S(1)} async-done(((bf16[16,3,4,1024]{3,2,1,0:T(4,128)(2,1)}), bf16[16,3,4,1024]{3,2,1,0:T(4,128)(2,1)S(1)}, u32[]{:S(2)}, u32[]{:S(2)}) %all-to-all-start.1) | async-done | bytes 393248 | tf_op jit(solution)/shard_map/all_to_all | solution.py:126
  53.8 0.1 copy.78
  53.9 0.8 reshape.245.rhs_ref.lhs_ref
  54.7 0.2 multiply_reduce_fusion.1
  55.0 0.6 mul.101.sub_ref
  55.6 16.7 %shard_map.77 = f32[3,1,1024]{2,1,0:T(1,128)} custom-call(s32[12]{0:T(128)} %reshape.248.valid_ref, bf16[4,64,1024]{2,1,0:T(8,128)(2,1)} %reshape.244.lhs_ref.rhs_ref, f32[4,1024,1]{2,1,0:T(8,128)} %copy.79.bias_ref, bf16[3,64,1024]{2,1,0:T(8,128)(2,1)} %reshape.245.rhs_ref.lhs_ref, f32[3,1,1024]{2,1,0:T(1,128)} %mul.101.sub_ref), custom_call_target="tpu_custom_call" | custom-call | tf_op jit(solution)/shard_map/pallas_call | solution.py:81
  72.3 0.8 broadcast_select_fusion
  73.1 17.1 %all_gather.7 = f32[16,3,1024]{2,1,0:T(4,128)S(1)} all-gather(f32[1,3,1024]{2,1,0:T(4,128)S(1)} %copy.80), channel_id=1, replica_groups=mesh['row'=32,'col'=16] {'col'}, dimensions={0}, use_global_device_ids=true | all-gather | bytes 208896 | tf_op jit(solution)/shard_map/all_gather | solution.py:151
  90.2 0.1 copy.81
  90.3 0.7 select_reduce_fusion.1
  91.0 0.8 select_reduce_fusion
  91.8 0.5 copy.85
  92.4 0.6 gather_fusion.2
  93.0 0.5 copy.83
  93.5 1.4 multiply_subtract_fusion.bias_ref
  94.9 16.9 %shard_map.78 = f32[4,1,1024]{2,1,0:T(1,128)} custom-call(s32[12]{0:T(128)} %reshape.250.valid_ref, bf16[3,64,1024]{2,1,0:T(8,128)(2,1)} %reshape.245.rhs_ref.lhs_ref, f32[3,1024,1]{2,1,0:T(8,128)} %multiply_subtract_fusion.bias_ref, bf16[4,64,1024]{2,1,0:T(8,128)(2,1)} %reshape.244.lhs_ref.rhs_ref, f32[4,1,1024]{2,1,0:T(1,128)} %mul.106.sub_ref), custom_call_target="tpu_custom_call" | custom-call | tf_op jit(solution)/shard_map/pallas_call | solution.py:81
  111.8 49.5 %all-gather = f32[128,1,1024]{2,1,0:T(1,128)S(1)} all-gather(f32[4,1,1024]{2,1,0:T(1,128)} %shard_map.78), channel_id=2, replica_groups=mesh['row'=32,'col'=16] {'row'}, dimensions={0}, use_global_device_ids=true | all-gather | bytes 540672 | tf_op jit(solution)/shard_map/all_gather | solution.py:166
  161.3 1.2 reduce.9
  162.5 0.1 reshape.276
  162.7 0.1 reduce_max.19
  162.8 0.2 exponential_reduce_fusion
  163.0 0.6 subtract_multiply_fusion.1
  (31 shorter events, 0.7 us)
Async XLA Ops:
  0.6 18.9 %copy-start = (bf16[16,4,1024]{2,1,0:T(4,128)(2,1)S(1)}, bf16[16,4,1024]{2,1,0:T(4,128)(2,1)}, u32[]{:S(2)}) copy-start(bf16[16,4,1024]{2,1,0:T(4,128)(2,1)} %param.6) | copy-start | bytes 393220
  2.7 30.2 %all-to-all-start = ((bf16[32,4,2,1024]{3,2,1,0:T(2,128)(2,1)}), bf16[32,4,2,1024]{3,2,1,0:T(2,128)(2,1)S(1)}, u32[]{:S(2)}, u32[]{:S(2)}) async-start(bf16[32,4,2,1024]{3,2,1,0:T(2,128)(2,1)} %broadcast_in_dim.102), calls=%async_computation | async-start | bytes 1048576 | tf_op jit(solution)/shard_map/all_to_all | solution.py:107
  20.7 22.9 %copy-start.3 = (f32[4,1024]{1,0:T(4,128)S(1)}, f32[4,1024]{1,0:T(4,128)}, u32[]{:S(2)}) copy-start(f32[4,1024]{1,0:T(4,128)} %param.11) | copy-start | bytes 49156
  32.9 20.8 %all-to-all-start.1 = ((bf16[16,3,4,1024]{3,2,1,0:T(4,128)(2,1)}), bf16[16,3,4,1024]{3,2,1,0:T(4,128)(2,1)S(1)}, u32[]{:S(2)}, u32[]{:S(2)}) async-start(bf16[16,3,4,1024]{3,2,1,0:T(4,128)(2,1)} %select_multiply_fusion), calls=%async_computation.1 | async-start | bytes 786432 | tf_op jit(solution)/shard_map/all_to_all | solution.py:126
  72.3 20.0 %copy-start.2 = (f32[16,1024]{1,0:T(8,128)S(1)}, f32[16,1024]{1,0:T(8,128)}, u32[]{:S(2)}) copy-start(f32[16,1024]{1,0:T(8,128)} %param.9) | copy-start | bytes 196612
  92.4 2.5 %copy-start.1 = (f32[16,1024]{1,0:T(8,128)}, f32[16,1024]{1,0:T(8,128)S(1)}, u32[]{:S(2)}) copy-start(f32[16,1024]{1,0:T(8,128)S(1)} %subtract_multiply_fusion) | copy-start | bytes 196612
  111.8 51.2 %copy-start.4 = (f32[4,1024]{1,0:T(4,128)S(1)}, f32[4,1024]{1,0:T(4,128)}, u32[]{:S(2)}) copy-start(f32[4,1024]{1,0:T(4,128)} %param.10) | copy-start | bytes 49156

commit v9 on v4

--- a/solution.py
+++ b/solution.py
@@ -146,7 +146,6 @@
     row_local = tile_lse(
         valid_int.reshape(-1), dst_full, dst_bias, src_four, (2.0 * src_sq)[:, None, :]
     )[:, 0, :]
-    row_local = jnp.where(my_ok[:, None], row_local, floor_value)
 
     row_all = lax.all_gather(row_local, "col", axis=0, tiled=False)
     owner = onehot.transpose(2, 0, 1)

time: 139 us -> 139 us (level)
  Pallas kernels: 36.2 us -> 33.5 us
  blocking collectives: 38.8 us -> 41.5 us
    all_to_all x1, blocking collectives: 22.4 us -> 25.9 us  [body(): col_all = lax.all_to_all(col_copies, 'row', 0, 0, tiled=True)]
    pallas_call x2, Pallas kernels: 36.2 us -> 33.5 us  [tile_lse(): pl.pallas_call(tile_kernel, grid_spec=grid_spec, out_shape=jax.ShapeDtype...]
where the time goes in v9:
time: 139 us; the launch traced here: 138 us
  blocking collectives  41.5 us (30%)
  Pallas kernels  33.5 us (24%)
  starting transfers between devices  20.6 us (15%)
  waiting for transfers between devices  18.7 us (13%)
  local copies, waits for them, and re-layouts  14.6 us (11%)
  other arithmetic  7.88 us (6%)
    pallas_call x2, Pallas kernels, tile_lse(): pl.pallas_call(tile_kernel, grid_spec=grid_spec, out_shape=jax.ShapeDtype...  33.5 us
    all_to_all x1, blocking collectives, body(): col_all = lax.all_to_all(col_copies, 'row', 0, 0, tiled=True)  25.9 us
    all_gather x1, blocking collectives, body(): row_all = lax.all_gather(row_local, 'col', axis=0, tiled=False)  15.6 us
    all_to_all x1, starting transfers between devices, body(): dst_recv = lax.all_to_all(dst_copies, 'row', 0, 0, tiled=True)  13.4 us
    all_to_all x1, waiting for transfers between devices, body(): dst_recv = lax.all_to_all(dst_copies, 'row', 0, 0, tiled=True)  11.2 us
    all_to_all x1, waiting for transfers between devices, body(): recv = lax.all_to_all(send, 'col', 0, 0, tiled=True)  7.54 us
    all_to_all x1, starting transfers between devices, body(): recv = lax.all_to_all(send, 'col', 0, 0, tiled=True)  7.21 us
  transfers between devices with their start and end apart: 2, of which 2 were waited for; matrix products, arithmetic and copies ran while one was open for 8% of the time, Pallas kernels for 0%

profile of v9, /device:TPU:6, one launch (start us, length us, event | category | flops | bytes accessed | tf_op | source)
XLA Modules:
  0.0 137.7 jit_solution(11001340530417353036)
XLA Ops:
  0.6 2.0 %broadcast_in_dim.95 = bf16[32,4,2,1024]{3,2,1,0:T(2,128)(2,1)} broadcast(bf16[4,2,1024]{2,1,0:T(2,128)(2,1)} %param.7), dimensions={1,2,3} | broadcast | bytes 540672 | tf_op jit(solution)/shard_map/broadcast_in_dim | solution.py:106
  2.7 13.4 %all-to-all-start = ((bf16[32,4,2,1024]{3,2,1,0:T(2,128)(2,1)}), bf16[32,4,2,1024]{3,2,1,0:T(2,128)(2,1)S(1)}, u32[]{:S(2)}, u32[]{:S(2)}) async-start(bf16[32,4,2,1024]{3,2,1,0:T(2,128)(2,1)} %broadcast_in_dim.95), calls=%async_computation | async-start | bytes 1048576 | tf_op jit(solution)/shard_map/all_to_all | solution.py:107
  16.1 0.8 copy.85
  16.8 0.7 add_select_fusion
  17.6 0.1 fusion
  17.9 0.2 select_reduce_fusion.2
  18.1 0.2 fusion.3
  18.3 0.2 dynamic-slice_reduce_fusion
  18.5 0.2 dynamic-slice_reduce_fusion.1
  18.7 0.1 reshape.210
  18.8 0.1 copy.86
  18.9 0.6 gather_fusion
  19.5 0.9 gather_fusion.1
  20.5 0.2 compare_reduce_fusion
  20.7 1.0 select_multiply_fusion
  21.8 11.2 %all-to-all-done = bf16[32,4,2,1024]{3,2,1,0:T(2,128)(2,1)S(1)} async-done(((bf16[32,4,2,1024]{3,2,1,0:T(2,128)(2,1)}), bf16[32,4,2,1024]{3,2,1,0:T(2,128)(2,1)S(1)}, u32[]{:S(2)}, u32[]{:S(2)}) %all-to-all-start) | async-done | bytes 524320 | tf_op jit(solution)/shard_map/all_to_all | solution.py:107
  32.9 7.2 %all-to-all-start.1 = ((bf16[16,3,4,1024]{3,2,1,0:T(4,128)(2,1)}), bf16[16,3,4,1024]{3,2,1,0:T(4,128)(2,1)S(1)}, u32[]{:S(2)}, u32[]{:S(2)}) async-start(bf16[16,3,4,1024]{3,2,1,0:T(4,128)(2,1)} %select_multiply_fusion), calls=%async_computation.1 | async-start | bytes 786432 | tf_op jit(solution)/shard_map/all_to_all | solution.py:126
  40.2 0.6 reshape.215.valid_ref
  40.8 0.1 fusion.11
  40.9 0.1 copy.92
  41.0 0.6 reshape.217.valid_ref
  41.6 0.4 copy.88
  42.0 1.0 reshape.211.lhs_ref.rhs_ref
  43.0 0.6 multiply_reduce_fusion
  43.6 2.0 %copy.90.bias_ref = f32[4,1024,1]{2,1,0:T(8,128)} copy(f32[4,1024,1]{1,0,2:T(4,128)S(1)} %get-tuple-element.9) | data formatting | bytes 32768 | tf_op jit(solution)/shard_map/broadcast_in_dim | solution.py:145
  45.6 0.6 mul.106.sub_ref
  46.2 7.5 %all-to-all-done.1 = bf16[16,3,4,1024]{3,2,1,0:T(4,128)(2,1)S(1)} async-done(((bf16[16,3,4,1024]{3,2,1,0:T(4,128)(2,1)}), bf16[16,3,4,1024]{3,2,1,0:T(4,128)(2,1)S(1)}, u32[]{:S(2)}, u32[]{:S(2)}) %all-to-all-start.1) | async-done | bytes 393248 | tf_op jit(solution)/shard_map/all_to_all | solution.py:126
  53.8 0.1 copy.89
  53.9 0.8 reshape.212.rhs_ref.lhs_ref
  54.7 0.2 multiply_reduce_fusion.1
  55.0 0.6 mul.101.sub_ref
  55.6 16.7 %shard_map.77 = f32[3,1,1024]{2,1,0:T(1,128)} custom-call(s32[12]{0:T(128)} %reshape.215.valid_ref, bf16[4,64,1024]{2,1,0:T(8,128)(2,1)} %reshape.211.lhs_ref.rhs_ref, f32[4,1024,1]{2,1,0:T(8,128)} %copy.90.bias_ref, bf16[3,64,1024]{2,1,0:T(8,128)(2,1)} %reshape.212.rhs_ref.lhs_ref, f32[3,1,1024]{2,1,0:T(1,128)} %mul.101.sub_ref), custom_call_target="tpu_custom_call" | custom-call | tf_op jit(solution)/shard_map/pallas_call | solution.py:81
  72.3 15.6 %all-gather = f32[48,1,1024]{2,1,0:T(1,128)S(1)} all-gather(f32[3,1,1024]{2,1,0:T(1,128)} %shard_map.77), channel_id=2, replica_groups=mesh['row'=32,'col'=16] {'col'}, dimensions={0}, use_global_device_ids=true | all-gather | bytes 208896 | tf_op jit(solution)/shard_map/all_gather | solution.py:150
  87.9 0.5 reduce.9
  88.5 0.1 copy.91
  88.6 0.7 select_reduce_fusion.1
  89.3 0.8 select_reduce_fusion
  90.1 0.5 copy.95
  90.7 0.6 gather_fusion.2
  91.3 0.5 copy.93
  91.8 1.4 %multiply_subtract_fusion.bias_ref = f32[3,1024,1]{2,1,0:T(8,128)} fusion(f32[3,1024,1]{2,1,0:T(8,128)S(1)} %copy.95, f32[3,1024,1]{2,1,0:T(8,128)S(1)} %copy.93, pred[3]{0:T(512)(128)(4,1)S(1)} %compare_and_fusion.1), kind=kLoop, calls=%fused_computation.5 | loop fusion | flops 9216 | bytes 36867 | tf_op jit(solution)/shard_map/sub | solution.py:160
  93.2 16.8 %shard_map.78 = f32[4,1,1024]{2,1,0:T(1,128)} custom-call(s32[12]{0:T(128)} %reshape.217.valid_ref, bf16[3,64,1024]{2,1,0:T(8,128)(2,1)} %reshape.212.rhs_ref.lhs_ref, f32[3,1024,1]{2,1,0:T(8,128)} %multiply_subtract_fusion.bias_ref, bf16[4,64,1024]{2,1,0:T(8,128)(2,1)} %reshape.211.lhs_ref.rhs_ref, f32[4,1,1024]{2,1,0:T(1,128)} %mul.106.sub_ref), custom_call_target="tpu_custom_call" | custom-call | tf_op jit(solution)/shard_map/pallas_call | solution.py:81
  110.0 0.7 copy.103
  110.8 0.1 broadcast_in_dim.106
  110.9 25.9 %all_to_all.15 = f32[32,4,1024]{2,1,0:T(4,128)S(1)} all-to-all(f32[32,4,1024]{2,1,0:T(4,128)S(1)} %broadcast_in_dim.106), channel_id=1, replica_groups=mesh['row'=32,'col'=16] {'row'}, dimensions={0} | all-to-all | bytes 1048576 | tf_op jit(solution)/shard_map/all_to_all | solution.py:166
  136.7 0.1 reduce_max.19
  136.8 0.2 exponential_reduce_fusion
  137.0 0.6 subtract_multiply_fusion.1
  (31 shorter events, 0.8 us)
Async XLA Ops:
  0.6 18.9 %copy-start = (bf16[16,4,1024]{2,1,0:T(4,128)(2,1)S(1)}, bf16[16,4,1024]{2,1,0:T(4,128)(2,1)}, u32[]{:S(2)}) copy-start(bf16[16,4,1024]{2,1,0:T(4,128)(2,1)} %param.6) | copy-start | bytes 393220
  2.7 30.2 %all-to-all-start = ((bf16[32,4,2,1024]{3,2,1,0:T(2,128)(2,1)}), bf16[32,4,2,1024]{3,2,1,0:T(2,128)(2,1)S(1)}, u32[]{:S(2)}, u32[]{:S(2)}) async-start(bf16[32,4,2,1024]{3,2,1,0:T(2,128)(2,1)} %broadcast_in_dim.95), calls=%async_computation | async-start | bytes 1048576 | tf_op jit(solution)/shard_map/all_to_all | solution.py:107
  20.7 22.9 %copy-start.3 = (f32[4,1024]{1,0:T(4,128)S(1)}, f32[4,1024]{1,0:T(4,128)}, u32[]{:S(2)}) copy-start(f32[4,1024]{1,0:T(4,128)} %param.11) | copy-start | bytes 49156
  32.9 20.8 %all-to-all-start.1 = ((bf16[16,3,4,1024]{3,2,1,0:T(4,128)(2,1)}), bf16[16,3,4,1024]{3,2,1,0:T(4,128)(2,1)S(1)}, u32[]{:S(2)}, u32[]{:S(2)}) async-start(bf16[16,3,4,1024]{3,2,1,0:T(4,128)(2,1)} %select_multiply_fusion), calls=%async_computation.1 | async-start | bytes 786432 | tf_op jit(solution)/shard_map/all_to_all | solution.py:126
  88.4 2.2 %copy-start.2 = (f32[16,1024]{1,0:T(8,128)S(1)}, f32[16,1024]{1,0:T(8,128)}, u32[]{:S(2)}) copy-start(f32[16,1024]{1,0:T(8,128)} %param.9) | copy-start | bytes 196612
  90.7 2.5 %copy-start.1 = (f32[16,1024]{1,0:T(8,128)}, f32[16,1024]{1,0:T(8,128)S(1)}, u32[]{:S(2)}) copy-start(f32[16,1024]{1,0:T(8,128)S(1)} %subtract_multiply_fusion) | copy-start | bytes 196612
  93.2 43.8 %copy-start.4 = (f32[4,1024]{1,0:T(4,128)S(1)}, f32[4,1024]{1,0:T(4,128)}, u32[]{:S(2)}) copy-start(f32[4,1024]{1,0:T(4,128)} %param.10) | copy-start | bytes 49156

commit v10 on v4

--- a/solution.py
+++ b/solution.py
@@ -13,7 +13,7 @@
 CHUNK = 256
 
 
-def tile_kernel(valid_ref, lhs_ref, bias_ref, rhs_ref, sub_ref, out_ref, acc_high, acc_total):
+def tile_kernel(valid_ref, lhs_ref, bias_ref, rhs_ref, sub_ref, out_ref, acc_high, acc_total, dense_bias):
     outer = pl.program_id(0)
     inner = pl.program_id(1)
     n_inner = pl.num_programs(1)
@@ -36,7 +36,11 @@
             vals = lax.dot_general(
                 left, rhs, (((0,), (0,)), ((), ())), preferred_element_type=jnp.float32
             )
-            vals = vals + bias_ref[0, pl.ds(start, CHUNK), :]
+            if dense_bias:
+                bias_row = jnp.broadcast_to(bias_ref[0, :, pl.ds(start, CHUNK)], (8, CHUNK))
+                vals = vals + jnp.transpose(bias_row)[:, 0:1]
+            else:
+                vals = vals + bias_ref[0, pl.ds(start, CHUNK), :]
             new_high = jnp.maximum(high, jnp.max(vals, axis=0, keepdims=True))
             total = total * jnp.exp(high - new_high) + jnp.sum(
                 jnp.exp(vals - new_high), axis=0, keepdims=True
@@ -63,7 +67,7 @@
         out_ref[0] = jnp.where(found, whole - sub_ref[0], floor_value)
 
 
-def tile_lse(valid, lhs, bias, rhs, sub):
+def tile_lse(valid, lhs, bias, rhs, sub, dense_bias=False):
     n_in, depth, reduced = lhs.shape
     n_out, _, kept = rhs.shape
     grid_spec = pltpu.PrefetchScalarGridSpec(
@@ -71,7 +75,7 @@
         grid=(n_out, n_in),
         in_specs=[
             pl.BlockSpec((1, depth, reduced), lambda o, n, v: (n, 0, 0)),
-            pl.BlockSpec((1, reduced, 1), lambda o, n, v: (n, 0, 0)),
+            pl.BlockSpec((1,) + bias.shape[1:], lambda o, n, v: (n, 0, 0)),
             pl.BlockSpec((1, depth, kept), lambda o, n, v: (o, 0, 0)),
             pl.BlockSpec((1, 1, kept), lambda o, n, v: (o, 0, 0)),
         ],
@@ -79,7 +83,7 @@
         scratch_shapes=[pltpu.VMEM((1, kept), jnp.float32), pltpu.VMEM((1, kept), jnp.float32)],
     )
     return pl.pallas_call(
-        tile_kernel,
+        functools.partial(tile_kernel, dense_bias=dense_bias),
         grid_spec=grid_spec,
         out_shape=jax.ShapeDtypeStruct((n_out, 1, kept), jnp.float32),
     )(valid, lhs, bias, rhs, sub)
@@ -158,9 +162,9 @@
     src_new = blur_scale * (log_src_mass - whole)
 
     my_pot = jnp.take(src_new, my_table, axis=0)
-    src_bias = (2.0 * my_pot - 2.0 * src_sq)[:, :, None]
+    src_bias = (2.0 * my_pot - 2.0 * src_sq)[:, None, :]
     col_local = tile_lse(
-        valid_int.T.reshape(-1), src_four, src_bias, dst_full, (2.0 * dst_sq)[:, None, :]
+        valid_int.T.reshape(-1), src_four, src_bias, dst_full, (2.0 * dst_sq)[:, None, :], True
     )[:, 0, :]
 
     col_copies = jnp.broadcast_to(col_local[None], (n_row,) + col_local.shape)

time: 139 us -> 140 us (level)
  blocking collectives: 38.8 us -> 44 us
  Pallas kernels: 36.2 us -> 33.3 us
    all_to_all x1, blocking collectives: 22.4 us -> 26.2 us  [body(): col_all = lax.all_to_all(col_copies, 'row', 0, 0, tiled=True)]
    pallas_call x2, Pallas kernels: 36.2 us -> 33.3 us  [tile_lse(): pl.pallas_call(functools.partial(tile_kernel, dense_bias=dense_bias), gri...]
where the time goes in v10:
time: 140 us; the launch traced here: 139 us
  blocking collectives  44 us (31%)
  Pallas kernels  33.3 us (24%)
  starting transfers between devices  20.7 us (15%)
  waiting for transfers between devices  18.7 us (13%)
  local copies, waits for them, and re-layouts  13.5 us (10%)
  other arithmetic  7.49 us (5%)
    pallas_call x2, Pallas kernels, tile_lse(): pl.pallas_call(functools.partial(tile_kernel, dense_bias=dense_bias), gri...  33.3 us
    all_to_all x1, blocking collectives, body(): col_all = lax.all_to_all(col_copies, 'row', 0, 0, tiled=True)  26.2 us
    all_gather x1, blocking collectives, body(): row_all = lax.all_gather(row_local, 'col', axis=0, tiled=False)  17.8 us
    all_to_all x1, starting transfers between devices, body(): dst_recv = lax.all_to_all(dst_copies, 'row', 0, 0, tiled=True)  13.5 us
    all_to_all x1, waiting for transfers between devices, body(): dst_recv = lax.all_to_all(dst_copies, 'row', 0, 0, tiled=True)  11.2 us
    all_to_all x1, waiting for transfers between devices, body(): recv = lax.all_to_all(send, 'col', 0, 0, tiled=True)  7.46 us
    all_to_all x1, starting transfers between devices, body(): recv = lax.all_to_all(send, 'col', 0, 0, tiled=True)  7.21 us
  transfers between devices with their start and end apart: 2, of which 2 were waited for; matrix products, arithmetic and copies ran while one was open for 8% of the time, Pallas kernels for 0%

profile of v10, /device:TPU:6, one launch (start us, length us, event | category | flops | bytes accessed | tf_op | source)
XLA Modules:
  0.0 138.5 jit_solution(14906657073412544837)
XLA Ops:
  0.6 2.0 %broadcast_in_dim.109 = bf16[32,4,2,1024]{3,2,1,0:T(2,128)(2,1)} broadcast(bf16[4,2,1024]{2,1,0:T(2,128)(2,1)} %param.7), dimensions={1,2,3} | broadcast | bytes 540672 | tf_op jit(solution)/shard_map/broadcast_in_dim | solution.py:110
  2.7 13.5 %all-to-all-start = ((bf16[32,4,2,1024]{3,2,1,0:T(2,128)(2,1)}), bf16[32,4,2,1024]{3,2,1,0:T(2,128)(2,1)S(1)}, u32[]{:S(2)}, u32[]{:S(2)}) async-start(bf16[32,4,2,1024]{3,2,1,0:T(2,128)(2,1)} %broadcast_in_dim.109), calls=%async_computation | async-start | bytes 1048576 | tf_op jit(solution)/shard_map/all_to_all | solution.py:111
  16.2 0.7 add_select_fusion
  16.9 0.8 copy.65
  17.7 0.1 fusion
  17.9 0.1 copy.63
  18.1 0.1 fusion.3
  18.2 0.2 select_reduce_fusion.2
  18.4 0.1 copy.67
  18.5 0.1 fusion.10
  18.6 0.2 dynamic-slice_reduce_fusion
  18.8 0.2 dynamic-slice_reduce_fusion.1
  19.0 0.1 copy.66
  19.1 0.1 reshape.235
  19.2 0.6 gather_fusion
  19.8 0.9 gather_fusion.1
  20.8 1.0 select_multiply_fusion
  21.8 11.2 %all-to-all-done = bf16[32,4,2,1024]{3,2,1,0:T(2,128)(2,1)S(1)} async-done(((bf16[32,4,2,1024]{3,2,1,0:T(2,128)(2,1)}), bf16[32,4,2,1024]{3,2,1,0:T(2,128)(2,1)S(1)}, u32[]{:S(2)}, u32[]{:S(2)}) %all-to-all-start) | async-done | bytes 524320 | tf_op jit(solution)/shard_map/all_to_all | solution.py:111
  33.0 7.2 %all-to-all-start.1 = ((bf16[16,3,4,1024]{3,2,1,0:T(4,128)(2,1)}), bf16[16,3,4,1024]{3,2,1,0:T(4,128)(2,1)S(1)}, u32[]{:S(2)}, u32[]{:S(2)}) async-start(bf16[16,3,4,1024]{3,2,1,0:T(4,128)(2,1)} %select_multiply_fusion), calls=%async_computation.1 | async-start | bytes 786432 | tf_op jit(solution)/shard_map/all_to_all | solution.py:130
  40.3 0.2 compare_reduce_fusion
  40.5 0.1 copy.73
  40.6 0.6 reshape.242.valid_ref
  41.3 0.6 reshape.240.valid_ref
  41.8 0.6 multiply_reduce_fusion
  42.4 0.6 mul.99.sub_ref
  43.1 0.4 copy.68
  43.4 1.0 reshape.236.lhs_ref.rhs_ref
  44.4 2.0 %copy.70.bias_ref = f32[4,1024,1]{2,1,0:T(8,128)} copy(f32[4,1024,1]{1,0,2:T(4,128)S(1)} %get-tuple-element.9) | data formatting | bytes 32768 | tf_op jit(solution)/shard_map/broadcast_in_dim | solution.py:149
  46.4 7.5 %all-to-all-done.1 = bf16[16,3,4,1024]{3,2,1,0:T(4,128)(2,1)S(1)} async-done(((bf16[16,3,4,1024]{3,2,1,0:T(4,128)(2,1)}), bf16[16,3,4,1024]{3,2,1,0:T(4,128)(2,1)S(1)}, u32[]{:S(2)}, u32[]{:S(2)}) %all-to-all-start.1) | async-done | bytes 393248 | tf_op jit(solution)/shard_map/all_to_all | solution.py:130
  53.9 0.2 multiply_reduce_fusion.1
  54.1 0.6 mul.95.sub_ref
  54.7 0.1 copy.69
  54.9 0.8 reshape.237.rhs_ref.lhs_ref
  55.7 15.7 %shard_map.77 = f32[3,1,1024]{2,1,0:T(1,128)} custom-call(s32[12]{0:T(128)} %reshape.240.valid_ref, bf16[4,64,1024]{2,1,0:T(8,128)(2,1)} %reshape.236.lhs_ref.rhs_ref, f32[4,1024,1]{2,1,0:T(8,128)} %copy.70.bias_ref, bf16[3,64,1024]{2,1,0:T(8,128)(2,1)} %reshape.237.rhs_ref.lhs_ref, f32[3,1,1024]{2,1,0:T(1,128)} %mul.95.sub_ref), custom_call_target="tpu_custom_call" | custom-call | tf_op jit(solution)/shard_map/pallas_call | solution.py:85
  71.4 0.8 broadcast_select_fusion.1
  72.2 17.8 %all_gather.4 = f32[16,3,1024]{2,1,0:T(4,128)S(1)} all-gather(f32[1,3,1024]{2,1,0:T(4,128)S(1)} %copy.71), channel_id=1, replica_groups=mesh['row'=32,'col'=16] {'col'}, dimensions={0}, use_global_device_ids=true | all-gather | bytes 208896 | tf_op jit(solution)/shard_map/all_gather | solution.py:155
  90.0 0.1 copy.72
  90.1 0.7 select_reduce_fusion.1
  90.8 0.8 select_reduce_fusion
  91.8 0.6 gather_fusion.2
  92.3 0.7 multiply_subtract_fusion.bias_ref
  93.0 17.6 %shard_map.78 = f32[4,1,1024]{2,1,0:T(1,128)} custom-call(s32[12]{0:T(128)} %reshape.242.valid_ref, bf16[3,64,1024]{2,1,0:T(8,128)(2,1)} %reshape.237.rhs_ref.lhs_ref, f32[3,1,1024]{2,1,0:T(1,128)} %multiply_subtract_fusion.bias_ref, bf16[4,64,1024]{2,1,0:T(8,128)(2,1)} %reshape.236.lhs_ref.rhs_ref, f32[4,1,1024]{2,1,0:T(1,128)} %mul.99.sub_ref), custom_call_target="tpu_custom_call" | custom-call | tf_op jit(solution)/shard_map/pallas_call | solution.py:85
  110.6 0.7 copy.80
  111.3 0.1 broadcast_in_dim.121
  111.5 26.2 %all_to_all.15 = f32[32,4,1024]{2,1,0:T(4,128)S(1)} all-to-all(f32[32,4,1024]{2,1,0:T(4,128)S(1)} %broadcast_in_dim.121), channel_id=1, replica_groups=mesh['row'=32,'col'=16] {'row'}, dimensions={0} | all-to-all | bytes 1048576 | tf_op jit(solution)/shard_map/all_to_all | solution.py:171
  137.6 0.1 reduce_max.19
  137.7 0.2 exponential_reduce_fusion
  137.9 0.6 subtract_multiply_fusion.1
  (29 shorter events, 0.5 us)
Async XLA Ops:
  0.6 19.1 %copy-start = (bf16[16,4,1024]{2,1,0:T(4,128)(2,1)S(1)}, bf16[16,4,1024]{2,1,0:T(4,128)(2,1)}, u32[]{:S(2)}) copy-start(bf16[16,4,1024]{2,1,0:T(4,128)(2,1)} %param.6) | copy-start | bytes 393220
  2.7 39.8 %copy-start.3 = (f32[4,1024]{1,0:T(4,128)S(1)}, f32[4,1024]{1,0:T(4,128)}, u32[]{:S(2)}) copy-start(f32[4,1024]{1,0:T(4,128)} %param.11) | copy-start | bytes 49156
  2.7 30.4 %all-to-all-start = ((bf16[32,4,2,1024]{3,2,1,0:T(2,128)(2,1)}), bf16[32,4,2,1024]{3,2,1,0:T(2,128)(2,1)S(1)}, u32[]{:S(2)}, u32[]{:S(2)}) async-start(bf16[32,4,2,1024]{3,2,1,0:T(2,128)(2,1)} %broadcast_in_dim.109), calls=%async_computation | async-start | bytes 1048576 | tf_op jit(solution)/shard_map/all_to_all | solution.py:111
  33.0 20.8 %all-to-all-start.1 = ((bf16[16,3,4,1024]{3,2,1,0:T(4,128)(2,1)}), bf16[16,3,4,1024]{3,2,1,0:T(4,128)(2,1)S(1)}, u32[]{:S(2)}, u32[]{:S(2)}) async-start(bf16[16,3,4,1024]{3,2,1,0:T(4,128)(2,1)} %select_multiply_fusion), calls=%async_computation.1 | async-start | bytes 786432 | tf_op jit(solution)/shard_map/all_to_all | solution.py:130
  55.7 35.9 %copy-start.2 = (f32[16,1024]{1,0:T(8,128)S(1)}, f32[16,1024]{1,0:T(8,128)}, u32[]{:S(2)}) copy-start(f32[16,1024]{1,0:T(8,128)} %param.9) | copy-start | bytes 196612
  91.6 46.3 %copy-start.4 = (f32[4,1024]{1,0:T(4,128)S(1)}, f32[4,1024]{1,0:T(4,128)}, u32[]{:S(2)}) copy-start(f32[4,1024]{1,0:T(4,128)} %param.10) | copy-start | bytes 49156
  91.7 46.8 %copy-start.1 = (f32[16,1024]{1,0:T(8,128)}, f32[16,1024]{1,0:T(8,128)S(1)}, u32[]{:S(2)}) copy-start(f32[16,1024]{1,0:T(8,128)S(1)} %subtract_multiply_fusion) | copy-start | bytes 196612

commit v11 on v10

--- a/solution.py
+++ b/solution.py
@@ -150,7 +150,6 @@
     row_local = tile_lse(
         valid_int.reshape(-1), dst_full, dst_bias, src_four, (2.0 * src_sq)[:, None, :]
     )[:, 0, :]
-    row_local = jnp.where(my_ok[:, None], row_local, floor_value)
 
     row_all = lax.all_gather(row_local, "col", axis=0, tiled=False)
     owner = onehot.transpose(2, 0, 1)

time: 140 us -> 141 us (level)
  Pallas kernels: 33.3 us -> 37.1 us
  blocking collectives: 44 us -> 41.3 us
    pallas_call x2, Pallas kernels: 33.3 us -> 37.1 us  [tile_lse(): pl.pallas_call(functools.partial(tile_kernel, dense_bias=dense_bias), gri...]
    all_gather x1, blocking collectives: 17.8 us -> 15.8 us  [body(): row_all = lax.all_gather(row_local, 'col', axis=0, tiled=False)]
where the time goes in v11:
time: 141 us; the launch traced here: 140 us
  blocking collectives  41.3 us (29%)
  Pallas kernels  37.1 us (26%)
  starting transfers between devices  20.7 us (15%)
  waiting for transfers between devices  18.7 us (13%)
  local copies, waits for them, and re-layouts  13.6 us (10%)
  other arithmetic  7.17 us (5%)
    pallas_call x2, Pallas kernels, tile_lse(): pl.pallas_call(functools.partial(tile_kernel, dense_bias=dense_bias), gri...  37.1 us
    all_to_all x1, blocking collectives, body(): col_all = lax.all_to_all(col_copies, 'row', 0, 0, tiled=True)  25.6 us
    all_gather x1, blocking collectives, body(): row_all = lax.all_gather(row_local, 'col', axis=0, tiled=False)  15.8 us
    all_to_all x1, starting transfers between devices, body(): dst_recv = lax.all_to_all(dst_copies, 'row', 0, 0, tiled=True)  13.5 us
    all_to_all x1, waiting for transfers between devices, body(): dst_recv = lax.all_to_all(dst_copies, 'row', 0, 0, tiled=True)  11.2 us
    all_to_all x1, waiting for transfers between devices, body(): recv = lax.all_to_all(send, 'col', 0, 0, tiled=True)  7.46 us
    all_to_all x1, starting transfers between devices, body(): recv = lax.all_to_all(send, 'col', 0, 0, tiled=True)  7.21 us
  transfers between devices with their start and end apart: 2, of which 2 were waited for; matrix products, arithmetic and copies ran while one was open for 8% of the time, Pallas kernels for 0%

profile of v11, /device:TPU:6, one launch (start us, length us, event | category | flops | bytes accessed | tf_op | source)
XLA Modules:
  0.0 139.5 jit_solution(7841930010963024393)
XLA Ops:
  0.6 2.0 %broadcast_in_dim.95 = bf16[32,4,2,1024]{3,2,1,0:T(2,128)(2,1)} broadcast(bf16[4,2,1024]{2,1,0:T(2,128)(2,1)} %param.7), dimensions={1,2,3} | broadcast | bytes 540672 | tf_op jit(solution)/shard_map/broadcast_in_dim | solution.py:110
  2.7 13.5 %all-to-all-start = ((bf16[32,4,2,1024]{3,2,1,0:T(2,128)(2,1)}), bf16[32,4,2,1024]{3,2,1,0:T(2,128)(2,1)S(1)}, u32[]{:S(2)}, u32[]{:S(2)}) async-start(bf16[32,4,2,1024]{3,2,1,0:T(2,128)(2,1)} %broadcast_in_dim.95), calls=%async_computation | async-start | bytes 1048576 | tf_op jit(solution)/shard_map/all_to_all | solution.py:111
  16.2 0.7 add_select_fusion
  16.9 0.8 copy.60
  17.7 0.1 fusion
  17.9 0.1 copy.58
  18.1 0.1 fusion.3
  18.2 0.2 select_reduce_fusion.2
  18.4 0.1 copy.62
  18.5 0.1 fusion.10
  18.6 0.2 dynamic-slice_reduce_fusion
  18.8 0.2 dynamic-slice_reduce_fusion.1
  19.0 0.1 copy.61
  19.1 0.1 reshape.201
  19.2 0.6 gather_fusion
  19.8 0.9 gather_fusion.1
  20.8 1.0 select_multiply_fusion
  21.8 11.2 %all-to-all-done = bf16[32,4,2,1024]{3,2,1,0:T(2,128)(2,1)S(1)} async-done(((bf16[32,4,2,1024]{3,2,1,0:T(2,128)(2,1)}), bf16[32,4,2,1024]{3,2,1,0:T(2,128)(2,1)S(1)}, u32[]{:S(2)}, u32[]{:S(2)}) %all-to-all-start) | async-done | bytes 524320 | tf_op jit(solution)/shard_map/all_to_all | solution.py:111
  33.0 7.2 %all-to-all-start.1 = ((bf16[16,3,4,1024]{3,2,1,0:T(4,128)(2,1)}), bf16[16,3,4,1024]{3,2,1,0:T(4,128)(2,1)S(1)}, u32[]{:S(2)}, u32[]{:S(2)}) async-start(bf16[16,3,4,1024]{3,2,1,0:T(4,128)(2,1)} %select_multiply_fusion), calls=%async_computation.1 | async-start | bytes 786432 | tf_op jit(solution)/shard_map/all_to_all | solution.py:130
  40.3 0.2 compare_reduce_fusion
  40.5 0.1 copy.67
  40.6 0.6 reshape.208.valid_ref
  41.3 0.6 reshape.206.valid_ref
  41.8 0.6 multiply_reduce_fusion
  42.4 0.6 mul.99.sub_ref
  43.1 0.4 copy.63
  43.4 1.0 reshape.202.lhs_ref.rhs_ref
  44.4 2.0 %copy.65.bias_ref = f32[4,1024,1]{2,1,0:T(8,128)} copy(f32[4,1024,1]{1,0,2:T(4,128)S(1)} %get-tuple-element.9) | data formatting | bytes 32768 | tf_op jit(solution)/shard_map/broadcast_in_dim | solution.py:149
  46.4 7.5 %all-to-all-done.1 = bf16[16,3,4,1024]{3,2,1,0:T(4,128)(2,1)S(1)} async-done(((bf16[16,3,4,1024]{3,2,1,0:T(4,128)(2,1)}), bf16[16,3,4,1024]{3,2,1,0:T(4,128)(2,1)S(1)}, u32[]{:S(2)}, u32[]{:S(2)}) %all-to-all-start.1) | async-done | bytes 393248 | tf_op jit(solution)/shard_map/all_to_all | solution.py:130
  53.9 0.2 multiply_reduce_fusion.1
  54.1 0.6 mul.95.sub_ref
  54.7 0.1 copy.64
  54.9 0.8 reshape.203.rhs_ref.lhs_ref
  55.7 17.2 %shard_map.77 = f32[3,1,1024]{2,1,0:T(1,128)} custom-call(s32[12]{0:T(128)} %reshape.206.valid_ref, bf16[4,64,1024]{2,1,0:T(8,128)(2,1)} %reshape.202.lhs_ref.rhs_ref, f32[4,1024,1]{2,1,0:T(8,128)} %copy.65.bias_ref, bf16[3,64,1024]{2,1,0:T(8,128)(2,1)} %reshape.203.rhs_ref.lhs_ref, f32[3,1,1024]{2,1,0:T(1,128)} %mul.95.sub_ref), custom_call_target="tpu_custom_call" | custom-call | tf_op jit(solution)/shard_map/pallas_call | solution.py:85
  72.9 15.8 %all-gather = f32[48,1,1024]{2,1,0:T(1,128)S(1)} all-gather(f32[3,1,1024]{2,1,0:T(1,128)} %shard_map.77), channel_id=2, replica_groups=mesh['row'=32,'col'=16] {'col'}, dimensions={0}, use_global_device_ids=true | all-gather | bytes 208896 | tf_op jit(solution)/shard_map/all_gather | solution.py:154
  88.7 0.5 reduce.9
  89.2 0.1 copy.66
  89.4 0.7 select_reduce_fusion.1
  90.0 0.8 select_reduce_fusion
  91.0 0.6 gather_fusion.2
  91.5 0.7 multiply_subtract_fusion.bias_ref
  92.2 20.0 %shard_map.78 = f32[4,1,1024]{2,1,0:T(1,128)} custom-call(s32[12]{0:T(128)} %reshape.208.valid_ref, bf16[3,64,1024]{2,1,0:T(8,128)(2,1)} %reshape.203.rhs_ref.lhs_ref, f32[3,1,1024]{2,1,0:T(1,128)} %multiply_subtract_fusion.bias_ref, bf16[4,64,1024]{2,1,0:T(8,128)(2,1)} %reshape.202.lhs_ref.rhs_ref, f32[4,1,1024]{2,1,0:T(1,128)} %mul.99.sub_ref), custom_call_target="tpu_custom_call" | custom-call | tf_op jit(solution)/shard_map/pallas_call | solution.py:85
  112.2 0.7 copy.75
  112.9 0.1 broadcast_in_dim.106
  113.0 25.6 %all_to_all.15 = f32[32,4,1024]{2,1,0:T(4,128)S(1)} all-to-all(f32[32,4,1024]{2,1,0:T(4,128)S(1)} %broadcast_in_dim.106), channel_id=1, replica_groups=mesh['row'=32,'col'=16] {'row'}, dimensions={0} | all-to-all | bytes 1048576 | tf_op jit(solution)/shard_map/all_to_all | solution.py:170
  138.6 0.1 reduce_max.19
  138.7 0.2 exponential_reduce_fusion
  138.9 0.6 subtract_multiply_fusion.1
  (29 shorter events, 0.6 us)
Async XLA Ops:
  0.6 19.1 %copy-start = (bf16[16,4,1024]{2,1,0:T(4,128)(2,1)S(1)}, bf16[16,4,1024]{2,1,0:T(4,128)(2,1)}, u32[]{:S(2)}) copy-start(bf16[16,4,1024]{2,1,0:T(4,128)(2,1)} %param.6) | copy-start | bytes 393220
  2.7 39.8 %copy-start.3 = (f32[4,1024]{1,0:T(4,128)S(1)}, f32[4,1024]{1,0:T(4,128)}, u32[]{:S(2)}) copy-start(f32[4,1024]{1,0:T(4,128)} %param.11) | copy-start | bytes 49156
  2.7 30.4 %all-to-all-start = ((bf16[32,4,2,1024]{3,2,1,0:T(2,128)(2,1)}), bf16[32,4,2,1024]{3,2,1,0:T(2,128)(2,1)S(1)}, u32[]{:S(2)}, u32[]{:S(2)}) async-start(bf16[32,4,2,1024]{3,2,1,0:T(2,128)(2,1)} %broadcast_in_dim.95), calls=%async_computation | async-start | bytes 1048576 | tf_op jit(solution)/shard_map/all_to_all | solution.py:111
  33.0 20.8 %all-to-all-start.1 = ((bf16[16,3,4,1024]{3,2,1,0:T(4,128)(2,1)}), bf16[16,3,4,1024]{3,2,1,0:T(4,128)(2,1)S(1)}, u32[]{:S(2)}, u32[]{:S(2)}) async-start(bf16[16,3,4,1024]{3,2,1,0:T(4,128)(2,1)} %select_multiply_fusion), calls=%async_computation.1 | async-start | bytes 786432 | tf_op jit(solution)/shard_map/all_to_all | solution.py:130
  72.9 18.0 %copy-start.2 = (f32[16,1024]{1,0:T(8,128)S(1)}, f32[16,1024]{1,0:T(8,128)}, u32[]{:S(2)}) copy-start(f32[16,1024]{1,0:T(8,128)} %param.9) | copy-start | bytes 196612
  90.9 48.0 %copy-start.4 = (f32[4,1024]{1,0:T(4,128)S(1)}, f32[4,1024]{1,0:T(4,128)}, u32[]{:S(2)}) copy-start(f32[4,1024]{1,0:T(4,128)} %param.10) | copy-start | bytes 49156
  91.0 48.6 %copy-start.1 = (f32[16,1024]{1,0:T(8,128)}, f32[16,1024]{1,0:T(8,128)S(1)}, u32[]{:S(2)}) copy-start(f32[16,1024]{1,0:T(8,128)S(1)} %subtract_multiply_fusion) | copy-start | bytes 196612
